TPU v7x, 512 devices: a whole 4x4x16 slice. The times are simulated.
512 devices in a mesh: band: 32 (over y, x, z_hi), slab: 16 (over z_lo, core).
Axes of the slice: x: 4, y: 4, z: 16 (z_hi: 2, z_lo: 8; z = z_hi * 8 + z_lo), core: 2. Of those that a mesh axis runs over, the one named last changes fastest.
Arguments:
- wave_coeffs: float32 [64, 2, 128, 128, 128], P('band', None, 'slab'), may hold values from -12 to 12
- column_mask: int32 [128, 128], replicated, may hold values from 0 to 1, as said below
- occupations: float32 [64], P('band'), may hold values from 0.1 to 2
- core_density: float32 [128, 128, 128], P('band', 'slab'), may hold values from 0.05 to 0.5
Outputs:
- hartree: float32 [128, 128, 128], P('band', 'slab')
- xc_potential: float32 [128, 128, 128], P('band', 'slab')
Inputs may be any that keep to these rules, and one draw needn't show every extreme that they name: `column_mask`: 1 marks a column of frequencies (first two indices) inside the cutoff; only columns whose shifted indices s1, s2 satisfy s1^2 + s2^2 <= 32^2 can be 1.
All inputs are finite; a program needn't handle non-finite values.
Results may differ from a plain program's by a relative error of at most 0.00035.
Values sent between devices are 32-bit elements; how exact they have to be, the bound alone decides.
No kernel may reach another device: no remote copies, remote signals or barrier semaphores. Data moves between devices by JAX's collectives and lax.ppermute only.
A program may use at most 64 MiB of HBM per device.

v0:
```python
import math

import jax
import jax.numpy as jnp
from jax import lax
from jax.sharding import PartitionSpec as P

grid_spacing = 0.59
wigner_a = 0.44
wigner_b = 7.8


def dft_tables(extent):
    indices = jnp.arange(extent, dtype=jnp.int32)
    phase = indices[:, None] * indices[None, :] % extent
    angle = phase.astype(jnp.float32) * (2.0 * math.pi / extent)
    return (jnp.cos(angle), jnp.sin(angle))


def kernel_block(extent, starts, amounts):
    pieces = []
    for offset, amount in zip(starts, amounts):
        frequency = offset + jnp.arange(amount, dtype=jnp.int32)
        shifted = (frequency + extent // 2) % extent - extent // 2
        pieces.append(shifted * shifted)
    squared = pieces[0][:, None, None] + pieces[1][None, :, None] + pieces[2][None, None, :]
    length = extent * grid_spacing
    scaled = length * length / math.pi / jnp.maximum(squared, 1).astype(jnp.float32)
    return jnp.where(squared == 0, 0.0, scaled)


def exchange_correlation(density):
    root_density = jnp.cbrt(density)
    radius = (3.0 / (4.0 * math.pi)) ** (1.0 / 3.0) / root_density
    exchange_part = -((3.0 / math.pi) ** (1.0 / 3.0)) * root_density
    shifted = radius + wigner_b
    correlation = -wigner_a / shifted - wigner_a * radius / (3.0 * shifted * shifted)
    return exchange_part + correlation


def project(pattern, values, matrix):
    return jnp.einsum(pattern, values, matrix, precision=lax.Precision.HIGHEST)


def rotate(real_part, imag_part, pattern, cosine_table, sine_table, direction):
    new_real = project(pattern, real_part, cosine_table) - direction * project(
        pattern, imag_part, sine_table
    )
    new_imag = direction * project(pattern, real_part, sine_table) + project(
        pattern, imag_part, cosine_table
    )
    return (new_real, new_imag)


def real_basis(extent):
    half = extent // 2
    indices = jnp.arange(extent, dtype=jnp.int32)
    frequency = jnp.where(indices <= half, indices, indices - half)
    phase = frequency[:, None] * indices[None, :] % extent
    angle = phase.astype(jnp.float32) * (2.0 * math.pi / extent)
    basis = jnp.where((indices <= half)[:, None], jnp.cos(angle), jnp.sin(angle))
    weight = jnp.where((indices == 0) | (indices == half), 1.0, 2.0).astype(jnp.float32)
    return basis, frequency, weight


def real_kernel_block(extent, frequency, weight, start, amount):
    rows = lax.dynamic_slice_in_dim(frequency, start, amount, 0)
    row_weight = lax.dynamic_slice_in_dim(weight, start, amount, 0)
    squared = (
        (rows * rows)[:, None, None]
        + (frequency * frequency)[None, :, None]
        + (frequency * frequency)[None, None, :]
    )
    length = extent * grid_spacing
    scaled = length * length / math.pi / jnp.maximum(squared, 1).astype(jnp.float32)
    kernel = jnp.where(squared == 0, 0.0, scaled)
    scale = row_weight[:, None, None] * weight[None, :, None] * weight[None, None, :]
    return kernel * scale / float(extent) ** 3


def local(wave_coeffs, column_mask, occupations, core_density):
    local_bands = wave_coeffs.shape[0]
    row_count = wave_coeffs.shape[2]
    extent = wave_coeffs.shape[3]
    band_count = lax.axis_size("band")
    bands_all = band_count * local_bands
    band_rows = extent // band_count
    slab_index = lax.axis_index("slab")
    cosine_table, sine_table = dft_tables(extent)
    mask_rows = lax.dynamic_slice_in_dim(column_mask, slab_index * row_count, row_count, 0).astype(
        jnp.float32
    )
    masked = wave_coeffs * mask_rows[None, None, :, :, None]
    real_part, imag_part = rotate(
        masked[:, 0], masked[:, 1], "bxyz,zw->bxyw", cosine_table, sine_table, 1.0
    )
    real_part, imag_part = rotate(
        real_part, imag_part, "bxyz,yw->bxwz", cosine_table, sine_table, 1.0
    )
    stacked = jnp.stack((real_part, imag_part), axis=1)
    arrived = lax.all_to_all(stacked, "slab", split_axis=3, concat_axis=2, tiled=True)
    plane_real, plane_imag = rotate(
        arrived[:, 0], arrived[:, 1], "bxyz,xw->bwyz", cosine_table, sine_table, 1.0
    )
    factor = 1.0 / (float(extent) ** 3 * bands_all)
    weights = occupations * factor
    partial_value = jnp.einsum(
        "b,bxyz->xyz",
        weights,
        plane_real * plane_real + plane_imag * plane_imag,
        precision=lax.Precision.HIGHEST,
    )
    basis, frequency, weight = real_basis(extent)
    spectrum = project("xyz,mz->xym", partial_value, basis)
    spectrum = project("xyz,mx->myz", spectrum, basis)
    arrived = lax.all_to_all(spectrum, "slab", split_axis=0, concat_axis=1, tiled=True)
    spectrum = project("xyz,my->xmz", arrived, basis)
    kernel = real_kernel_block(extent, frequency, weight, slab_index * row_count, row_count)
    potential = project("xmz,my->xyz", kernel * spectrum, basis)
    arrived = lax.all_to_all(potential, "slab", split_axis=1, concat_axis=0, tiled=True)
    potential = project("myz,mx->xyz", arrived, basis)
    partial_hartree = project("xym,mz->xyz", potential, basis)
    both = jnp.stack((partial_value, partial_hartree)).reshape(
        2, band_count, band_rows, row_count, extent
    )
    summed = lax.all_to_all(both, "band", split_axis=1, concat_axis=1, tiled=True).sum(axis=1)
    own_density, hartree = summed[0], summed[1]
    xc_potential = exchange_correlation(own_density + core_density)
    return (hartree, xc_potential)


def solution(mesh):
    return jax.shard_map(
        local,
        mesh=mesh,
        in_specs=(P("band", None, "slab", None, None), P(), P("band"), P("band", "slab", None)),
        out_specs=(P("band", "slab", None), P("band", "slab", None)),
        check_vma=False,
    )
```

profile of v0, /device:TPU:33, one launch (start us, length us, event | category | flops | bytes accessed | tf_op | source)
XLA Modules:
  0.0 280.5 jit_solution(254616200782747427)
XLA Ops:
  0.6 0.7 dynamic-slice_convert_fusion
  1.3 1.9 copy_multiply_fusion
  3.2 1.2 fusion.11
  4.4 1.2 fusion.12
  5.7 1.2 convolution_subtract_fusion.2
  6.9 1.3 fusion.49
  8.2 1.3 fusion.40
  9.5 1.2 convolution_add_fusion.2
  10.7 1.3 fusion.5
  12.0 1.3 fusion.4
  13.4 0.2 pad_maximum_fusion
  13.6 2.5 copy.48
  16.1 12.9 %all-to-all-start = ((f32[2,2,8,128,128]{4,2,0,1,3:T(8,128)}), f32[2,2,8,128,128]{4,2,0,1,3:T(8,128)S(1)}, u32[]{:S(2)}, u32[]{:S(2)}) async-start(f32[2,2,8,128,128]{4,2,0,1,3:T(8,128)} %copy.48), calls=%async_computation | async-start | bytes 4194304 | tf_op jit(solution)/shard_map/all_to_all | solution.py:101
  29.1 90.3 %all-to-all-done = f32[2,2,8,128,128]{4,2,0,1,3:T(8,128)S(1)} async-done(((f32[2,2,8,128,128]{4,2,0,1,3:T(8,128)}), f32[2,2,8,128,128]{4,2,0,1,3:T(8,128)S(1)}, u32[]{:S(2)}, u32[]{:S(2)}) %all-to-all-start) | async-done | bytes 2097184 | tf_op jit(solution)/shard_map/all_to_all | solution.py:101
  119.4 1.2 copy.50
  120.6 0.1 fusion.151
  120.7 1.3 fusion.10
  122.1 1.3 fusion.9
  123.4 1.4 fusion.3
  124.8 0.0 copy-start.1
  124.8 1.4 fusion.2
  126.2 0.0 copy-done.1
  126.2 4.1 %fusion.7 = f32[1,128,8,128]{3,0,2,1:T(1,128)S(1)} fusion(f32[2,128,8,128]{3,1,2,0:T(8,128)S(1)} %fusion.2, f32[2]{0:T(128)S(1)} %copy-done.1), kind=kOutput, calls=%fused_computation.22 | convolution fusion | flops 3145730 | bytes 1572872 | tf_op jit(solution)/shard_map/b,bxyz->xyz/dot_general | solution.py:107
  130.3 0.9 fusion.22
  131.2 0.9 fusion.33
  132.1 1.1 copy.58
  133.2 8.6 %all-to-all-start.1 = ((f32[128,8,128]{2,1,0:T(8,128)}), f32[128,8,128]{2,1,0:T(8,128)S(1)}, u32[]{:S(2)}, u32[]{:S(2)}) async-start(f32[128,8,128]{2,1,0:T(8,128)} %copy.58), calls=%async_computation.1 | async-start | bytes 1048576 | tf_op jit(solution)/shard_map/all_to_all | solution.py:116
  141.8 0.1 dynamic_slice.11
  141.9 0.1 dynamic-slice_multiply_fusion
  142.0 0.1 broadcast_multiply_fusion
  142.0 0.1 broadcast_add_fusion
  142.1 26.5 %all-to-all-done.1 = f32[128,8,128]{2,1,0:T(8,128)S(1)} async-done(((f32[128,8,128]{2,1,0:T(8,128)}), f32[128,8,128]{2,1,0:T(8,128)S(1)}, u32[]{:S(2)}, u32[]{:S(2)}) %all-to-all-start.1) | async-done | bytes 524320 | tf_op jit(solution)/shard_map/all_to_all | solution.py:116
  168.6 0.9 fusion.6
  169.5 0.9 convolution_bitcast_fusion
  170.5 0.3 copy.61
  170.8 33.1 %all_to_all.59 = f32[8,128,128]{2,0,1:T(8,128)S(1)} all-to-all(f32[8,128,128]{2,0,1:T(8,128)S(1)} %copy.61), channel_id=1, replica_groups=mesh['band'=32,'slab'=16] {'slab'}, dimensions={1} | all-to-all | bytes 1048576 | tf_op jit(solution)/shard_map/all_to_all | solution.py:120
  203.9 0.1 copy.63
  204.0 1.0 fusion.19
  204.9 0.9 fusion.30
  205.8 0.3 copy.66
  206.1 0.1 pad_maximum_fusion.1
  206.2 0.3 copy.67
  206.5 0.0 copy-start
  206.5 72.5 %all_to_all.60 = f32[2,32,4,8,128]{4,2,3,0,1:T(4,128)S(1)} all-to-all(f32[2,32,4,8,128]{4,2,3,0,1:T(4,128)S(1)} %copy.67), channel_id=1, replica_groups=mesh['band'=32,'slab'=16] {'band'}, dimensions={1} | all-to-all | bytes 2097152 | tf_op jit(solution)/shard_map/all_to_all | solution.py:126
  279.1 0.2 reduce_sum.9
  279.3 0.6 copy.70
  279.9 0.0 copy-done
  279.9 0.1 fusion.72
  279.9 0.6 copy.71
  (5 shorter events, 0.0 us)
Async XLA Ops:
  16.1 103.2 %all-to-all-start = ((f32[2,2,8,128,128]{4,2,0,1,3:T(8,128)}), f32[2,2,8,128,128]{4,2,0,1,3:T(8,128)S(1)}, u32[]{:S(2)}, u32[]{:S(2)}) async-start(f32[2,2,8,128,128]{4,2,0,1,3:T(8,128)} %copy.48), calls=%async_computation | async-start | bytes 4194304 | tf_op jit(solution)/shard_map/all_to_all | solution.py:101
  124.8 1.4 copy-start.1
  133.2 35.4 %all-to-all-start.1 = ((f32[128,8,128]{2,1,0:T(8,128)}), f32[128,8,128]{2,1,0:T(8,128)S(1)}, u32[]{:S(2)}, u32[]{:S(2)}) async-start(f32[128,8,128]{2,1,0:T(8,128)} %copy.58), calls=%async_computation.1 | async-start | bytes 1048576 | tf_op jit(solution)/shard_map/all_to_all | solution.py:116
  206.5 73.3 %copy-start = (f32[4,8,128]{2,1,0:T(8,128)S(1)}, f32[4,8,128]{2,1,0:T(8,128)}, u32[]{:S(2)}) copy-start(f32[4,8,128]{2,1,0:T(8,128)} %param.7) | copy-start | bytes 49156
where the time goes:
time: 281 us
  waiting for transfers between devices  117 us (42%)
  blocking collectives  106 us (38%)
  matrix products  25.1 us (9%)
  starting transfers between devices  21.5 us (8%)
  local copies, waits for them, and re-layouts  7.36 us (3%)
  other arithmetic  3.33 us (1%)
    all_to_all x1, waiting for transfers between devices, local(): lax.all_to_all(stacked, 'slab', split_axis=3, concat_axis=2, tiled=True)  90.3 us
    all_to_all x1, blocking collectives, local(): lax.all_to_all(both, 'band', split_axis=1, concat_axis=1, tiled=True)  72.5 us
    all_to_all x1, blocking collectives, local(): lax.all_to_all(potential, 'slab', split_axis=1, concat_axis=0, tiled=True)  33.1 us
    all_to_all x1, waiting for transfers between devices, local(): lax.all_to_all(spectrum, 'slab', split_axis=0, concat_axis=1, tiled=True)  26.5 us
    dot_general x18, matrix products, project(): return jnp.einsum(pattern, values, matrix, precision=lax.Precision.HIGHEST)  21 us
    all_to_all x1, starting transfers between devices, local(): lax.all_to_all(stacked, 'slab', split_axis=3, concat_axis=2, tiled=True)  12.9 us
    all_to_all x1, starting transfers between devices, local(): lax.all_to_all(spectrum, 'slab', split_axis=0, concat_axis=1, tiled=True)  8.61 us
  transfers between devices with their start and end apart: 2, of which 2 were waited for; matrix products, arithmetic and copies ran while one was open for 0% of the time, Pallas kernels for 0%

commit v1 on v0

--- a/solution.py
+++ b/solution.py
@@ -78,6 +78,13 @@
     return kernel * scale / float(extent) ** 3
 
 
+def support(values, axis, half_width):
+    extent = values.shape[axis]
+    low = lax.slice_in_dim(values, 0, half_width, axis=axis)
+    high = lax.slice_in_dim(values, extent - half_width, extent, axis=axis)
+    return jnp.concatenate((low, high), axis=axis)
+
+
 def local(wave_coeffs, column_mask, occupations, core_density):
     local_bands = wave_coeffs.shape[0]
     row_count = wave_coeffs.shape[2]
@@ -86,45 +93,51 @@
     bands_all = band_count * local_bands
     band_rows = extent // band_count
     slab_index = lax.axis_index("slab")
+    half_width = -(-(extent // 4 + 1) // 4) * 4
     cosine_table, sine_table = dft_tables(extent)
-    mask_rows = lax.dynamic_slice_in_dim(column_mask, slab_index * row_count, row_count, 0).astype(
-        jnp.float32
-    )
-    masked = wave_coeffs * mask_rows[None, None, :, :, None]
+    cosine_kept = support(cosine_table, 0, half_width)
+    sine_kept = support(sine_table, 0, half_width)
+    mask_rows = lax.dynamic_slice_in_dim(column_mask, slab_index * row_count, row_count, 0)
+    mask_kept = support(mask_rows, 1, half_width).astype(jnp.float32)
+    masked = support(wave_coeffs, 3, half_width) * mask_kept[None, None, :, :, None]
     real_part, imag_part = rotate(
-        masked[:, 0], masked[:, 1], "bxyz,zw->bxyw", cosine_table, sine_table, 1.0
-    )
-    real_part, imag_part = rotate(
-        real_part, imag_part, "bxyz,yw->bxwz", cosine_table, sine_table, 1.0
+        masked[:, 0], masked[:, 1], "bxyz,zw->bwxy", cosine_table, sine_table, 1.0
     )
     stacked = jnp.stack((real_part, imag_part), axis=1)
-    arrived = lax.all_to_all(stacked, "slab", split_axis=3, concat_axis=2, tiled=True)
+    arrived = lax.all_to_all(stacked, "slab", split_axis=2, concat_axis=3, tiled=True)
+    arrived = support(arrived, 3, half_width)
+    real_part, imag_part = rotate(
+        arrived[:, 0], arrived[:, 1], "bzxy,xw->bzwy", cosine_kept, sine_kept, 1.0
+    )
     plane_real, plane_imag = rotate(
-        arrived[:, 0], arrived[:, 1], "bxyz,xw->bwyz", cosine_table, sine_table, 1.0
+        real_part, imag_part, "bzxy,yw->bzxw", cosine_kept, sine_kept, 1.0
     )
     factor = 1.0 / (float(extent) ** 3 * bands_all)
     weights = occupations * factor
     partial_value = jnp.einsum(
-        "b,bxyz->xyz",
+        "b,bzxy->zxy",
         weights,
         plane_real * plane_real + plane_imag * plane_imag,
         precision=lax.Precision.HIGHEST,
     )
     basis, frequency, weight = real_basis(extent)
-    spectrum = project("xyz,mz->xym", partial_value, basis)
-    spectrum = project("xyz,mx->myz", spectrum, basis)
-    arrived = lax.all_to_all(spectrum, "slab", split_axis=0, concat_axis=1, tiled=True)
-    spectrum = project("xyz,my->xmz", arrived, basis)
+    spectrum = project("zxy,mx->zmy", partial_value, basis)
+    spectrum = project("zxy,my->zxm", spectrum, basis)
+    arrived = lax.all_to_all(spectrum, "slab", split_axis=1, concat_axis=0, tiled=True)
+    spectrum = project("zxy,mz->mxy", arrived, basis)
     kernel = real_kernel_block(extent, frequency, weight, slab_index * row_count, row_count)
-    potential = project("xmz,my->xyz", kernel * spectrum, basis)
-    arrived = lax.all_to_all(potential, "slab", split_axis=1, concat_axis=0, tiled=True)
-    potential = project("myz,mx->xyz", arrived, basis)
-    partial_hartree = project("xym,mz->xyz", potential, basis)
+    kernel = jnp.transpose(kernel, (2, 0, 1))
+    potential = project("mxy,mz->zxy", kernel * spectrum, basis)
+    arrived = lax.all_to_all(potential, "slab", split_axis=0, concat_axis=1, tiled=True)
+    potential = project("zmy,mx->zxy", arrived, basis)
+    partial_hartree = project("zxm,my->zxy", potential, basis)
     both = jnp.stack((partial_value, partial_hartree)).reshape(
-        2, band_count, band_rows, row_count, extent
+        2, row_count, band_count, band_rows, extent
     )
-    summed = lax.all_to_all(both, "band", split_axis=1, concat_axis=1, tiled=True).sum(axis=1)
-    own_density, hartree = summed[0], summed[1]
+    summed = lax.all_to_all(both, "band", split_axis=2, concat_axis=2, tiled=True).sum(axis=2)
+    placed = lax.all_to_all(summed, "slab", split_axis=3, concat_axis=1, tiled=True)
+    placed = jnp.transpose(placed, (0, 2, 3, 1))
+    own_density, hartree = placed[0], placed[1]
     xc_potential = exchange_correlation(own_density + core_density)
     return (hartree, xc_potential)
 

time: 281 us -> 299 us (1.064)
  the two profiles are of different devices: /device:TPU:33 before, /device:TPU:1 now
where the time goes in v1:
time: 299 us
  waiting for transfers between devices  132 us (44%)
  blocking collectives  88.6 us (30%)
  starting transfers between devices  38.9 us (13%)
  matrix products  24.1 us (8%)
  local copies, waits for them, and re-layouts  10.9 us (4%)
    all_to_all x1, waiting for transfers between devices, local(): lax.all_to_all(stacked, 'slab', split_axis=2, concat_axis=3, tiled=True)  80.6 us
    all_to_all x1, blocking collectives, local(): lax.all_to_all(summed, 'slab', split_axis=3, concat_axis=1, tiled=True)  44.8 us
    all_to_all x1, blocking collectives, local(): lax.all_to_all(both, 'band', split_axis=2, concat_axis=2, tiled=True)  43.8 us
    all_to_all x1, waiting for transfers between devices, local(): lax.all_to_all(spectrum, 'slab', split_axis=1, concat_axis=0, tiled=True)  25.9 us
    all_to_all x1, waiting for transfers between devices, local(): lax.all_to_all(potential, 'slab', split_axis=0, concat_axis=1, tiled=True)  25.9 us
    dot_general x18, matrix products, project(): return jnp.einsum(pattern, values, matrix, precision=lax.Precision.HIGHEST)  20.1 us
    all_to_all x1, starting transfers between devices, local(): lax.all_to_all(spectrum, 'slab', split_axis=1, concat_axis=0, tiled=True)  17.8 us
    all_to_all x1, starting transfers between devices, local(): lax.all_to_all(stacked, 'slab', split_axis=2, concat_axis=3, tiled=True)  14 us
  transfers between devices with their start and end apart: 3, of which 3 were waited for; matrix products, arithmetic and copies ran while one was open for 0% of the time, Pallas kernels for 0%

profile of v1, /device:TPU:1, one launch (start us, length us, event | category | flops | bytes accessed | tf_op | source)
XLA Modules:
  0.0 298.7 jit_solution(12740885639891986372)
XLA Ops:
  0.6 0.0 copy-start
  0.6 0.8 copy-done
  1.5 0.1 fusion.120
  1.6 1.4 fusion.117
  2.9 0.1 add_convert_fusion
  3.0 0.2 copy_multiply_fusion
  3.2 0.9 fusion.13
  4.1 0.9 fusion.12
  5.0 0.9 fusion.6
  5.9 0.9 fusion.5
  6.8 0.1 pad_maximum_fusion.1
  6.9 2.0 copy.39
  8.9 14.0 %all-to-all-start = ((f32[2,2,128,8,72]{4,3,0,1,2:T(8,128)}), f32[2,2,128,8,72]{4,3,0,1,2:T(8,128)S(1)}, u32[]{:S(2)}, u32[]{:S(2)}) async-start(f32[2,2,128,8,72]{4,3,0,1,2:T(8,128)} %copy.39), calls=%async_computation | async-start | bytes 4194304 | tf_op jit(solution)/shard_map/all_to_all | solution.py:107
  23.0 0.3 fusion.52
  23.2 0.3 fusion.53
  23.5 80.6 %all-to-all-done = f32[2,2,128,8,72]{4,3,0,1,2:T(8,128)S(1)} async-done(((f32[2,2,128,8,72]{4,3,0,1,2:T(8,128)}), f32[2,2,128,8,72]{4,3,0,1,2:T(8,128)S(1)}, u32[]{:S(2)}, u32[]{:S(2)}) %all-to-all-start) | async-done | bytes 1179680 | tf_op jit(solution)/shard_map/all_to_all | solution.py:107
  104.1 0.2 copy.96
  104.3 0.1 fusion.116
  104.5 0.4 copy.80
  104.9 0.4 copy.81
  105.3 0.2 fusion.11
  105.6 0.7 fusion.48
  106.2 0.7 fusion.50
  106.9 0.6 fusion.4
  107.5 1.8 fusion.64
  109.4 1.8 fusion.63
  111.2 0.6 fusion.3
  111.8 1.8 fusion.2
  113.7 0.0 copy-start.2
  113.7 1.8 fusion.1
  115.5 4.0 %fusion.7 = f32[1,8,128,128]{3,0,2,1:T(1,128)S(1)} fusion(f32[2,8,128,128]{3,2,1,0:T(8,128)S(1)} %fusion.1, f32[2]{0:T(128)S(1)} %copy-done.2), kind=kOutput, calls=%fused_computation.23 | convolution fusion | flops 3145730 | bytes 1572872 | tf_op jit(solution)/shard_map/b,bzxy->zxy/dot_general | solution.py:117
  119.5 0.9 convolution_bitcast_fusion.1
  120.4 1.9 fusion.20
  122.3 17.8 %all-to-all-start.1 = ((f32[8,128,128]{2,0,1:T(8,128)}), f32[8,128,128]{2,0,1:T(8,128)S(1)}, u32[]{:S(2)}, u32[]{:S(2)}) async-start(f32[8,128,128]{2,0,1:T(8,128)} %fusion.20), calls=%async_computation.1 | async-start | bytes 1048576 | tf_op jit(solution)/shard_map/all_to_all | solution.py:126
  140.1 0.1 dynamic_slice.11
  140.2 0.1 dynamic-slice_multiply_fusion
  140.3 0.1 broadcast_multiply_fusion
  140.3 0.1 broadcast_add_fusion
  140.4 25.9 %all-to-all-done.1 = f32[8,128,128]{2,0,1:T(8,128)S(1)} async-done(((f32[8,128,128]{2,0,1:T(8,128)}), f32[8,128,128]{2,0,1:T(8,128)S(1)}, u32[]{:S(2)}, u32[]{:S(2)}) %all-to-all-start.1) | async-done | bytes 524320 | tf_op jit(solution)/shard_map/all_to_all | solution.py:126
  166.3 0.1 copy.47
  166.4 1.0 convolution_multiply_fusion
  167.5 0.9 fusion.35
  168.4 1.1 copy.50
  169.5 7.1 %all-to-all-start.2 = ((f32[128,8,128]{2,1,0:T(8,128)}), f32[128,8,128]{2,1,0:T(8,128)S(1)}, u32[]{:S(2)}, u32[]{:S(2)}) async-start(f32[128,8,128]{2,1,0:T(8,128)} %copy.50), calls=%async_computation.2 | async-start | bytes 1048576 | tf_op jit(solution)/shard_map/all_to_all | solution.py:131
  176.6 0.3 copy.65
  176.9 25.9 %all-to-all-done.2 = f32[128,8,128]{2,1,0:T(8,128)S(1)} async-done(((f32[128,8,128]{2,1,0:T(8,128)}), f32[128,8,128]{2,1,0:T(8,128)S(1)}, u32[]{:S(2)}, u32[]{:S(2)}) %all-to-all-start.2) | async-done | bytes 524320 | tf_op jit(solution)/shard_map/all_to_all | solution.py:131
  202.8 0.9 convolution_bitcast_fusion
  203.8 0.9 fusion.30
  204.7 0.3 copy.53
  205.0 0.1 pad_maximum_fusion.2
  205.1 0.3 copy.54
  205.4 43.8 %all_to_all.77 = f32[2,8,32,4,128]{4,3,1,0,2:T(4,128)S(1)} all-to-all(f32[2,8,32,4,128]{4,3,1,0,2:T(4,128)S(1)} %copy.54), channel_id=1, replica_groups=mesh['band'=32,'slab'=16] {'band'}, dimensions={2} | all-to-all | bytes 2097152 | tf_op jit(solution)/shard_map/all_to_all | solution.py:137
  249.2 0.2 reduce_sum.9
  249.4 0.3 copy.56
  249.6 0.5 reshape.144
  250.2 0.0 copy-start.1
  250.2 44.8 %all_to_all.78 = f32[16,1,512]{2,1,0:T(1,128)S(1)} all-to-all(f32[16,1,512]{2,1,0:T(1,128)S(1)} %reshape.144), channel_id=1, replica_groups=mesh['band'=32,'slab'=16] {'slab'}, dimensions={0} | all-to-all | bytes 65536 | tf_op jit(solution)/shard_map/all_to_all | solution.py:138
  295.0 0.5 broadcast.226
  295.5 0.7 reduce
  296.2 0.6 reshape.145
  296.9 0.3 copy.97
  297.2 0.3 all_to_all.71
  297.4 0.6 slice_bitcast_fusion.7
  298.0 0.7 fusion.60
  (9 shorter events, 0.0 us)
Async XLA Ops:
  0.6 0.8 copy-start
  8.9 95.2 %all-to-all-start = ((f32[2,2,128,8,72]{4,3,0,1,2:T(8,128)}), f32[2,2,128,8,72]{4,3,0,1,2:T(8,128)S(1)}, u32[]{:S(2)}, u32[]{:S(2)}) async-start(f32[2,2,128,8,72]{4,3,0,1,2:T(8,128)} %copy.39), calls=%async_computation | async-start | bytes 4194304 | tf_op jit(solution)/shard_map/all_to_all | solution.py:107
  113.7 1.9 copy-start.2
  122.3 44.0 %all-to-all-start.1 = ((f32[8,128,128]{2,0,1:T(8,128)}), f32[8,128,128]{2,0,1:T(8,128)S(1)}, u32[]{:S(2)}, u32[]{:S(2)}) async-start(f32[8,128,128]{2,0,1:T(8,128)} %fusion.20), calls=%async_computation.1 | async-start | bytes 1048576 | tf_op jit(solution)/shard_map/all_to_all | solution.py:126
  169.5 33.3 %all-to-all-start.2 = ((f32[128,8,128]{2,1,0:T(8,128)}), f32[128,8,128]{2,1,0:T(8,128)S(1)}, u32[]{:S(2)}, u32[]{:S(2)}) async-start(f32[128,8,128]{2,1,0:T(8,128)} %copy.50), calls=%async_computation.2 | async-start | bytes 1048576 | tf_op jit(solution)/shard_map/all_to_all | solution.py:131
  250.2 47.9 %copy-start.1 = (f32[4,8,128]{2,1,0:T(8,128)S(1)}, f32[4,8,128]{2,1,0:T(8,128)}, u32[]{:S(2)}) copy-start(f32[4,8,128]{2,1,0:T(8,128)} %param.7) | copy-start | bytes 49156

commit v2 on v1

--- a/solution.py
+++ b/solution.py
@@ -3,7 +3,7 @@
 import jax
 import jax.numpy as jnp
 from jax import lax
-from jax.sharding import PartitionSpec as P
+from jax.sharding import Mesh, PartitionSpec as P
 
 grid_spacing = 0.59
 wigner_a = 0.44
@@ -89,9 +89,12 @@
     local_bands = wave_coeffs.shape[0]
     row_count = wave_coeffs.shape[2]
     extent = wave_coeffs.shape[3]
-    band_count = lax.axis_size("band")
+    plane_count = lax.axis_size("plane")
+    half_count = lax.axis_size("half")
+    band_count = plane_count * half_count
     bands_all = band_count * local_bands
     band_rows = extent // band_count
+    slab_count = lax.axis_size("slab")
     slab_index = lax.axis_index("slab")
     half_width = -(-(extent // 4 + 1) // 4) * 4
     cosine_table, sine_table = dft_tables(extent)
@@ -101,13 +104,19 @@
     mask_kept = support(mask_rows, 1, half_width).astype(jnp.float32)
     masked = support(wave_coeffs, 3, half_width) * mask_kept[None, None, :, :, None]
     real_part, imag_part = rotate(
-        masked[:, 0], masked[:, 1], "bxyz,zw->bwxy", cosine_table, sine_table, 1.0
+        masked[:, 0], masked[:, 1], "bxyz,zw->wbxy", cosine_table, sine_table, 1.0
     )
-    stacked = jnp.stack((real_part, imag_part), axis=1)
-    arrived = lax.all_to_all(stacked, "slab", split_axis=2, concat_axis=3, tiled=True)
-    arrived = support(arrived, 3, half_width)
+    stacked = jnp.stack((real_part, imag_part), axis=2).reshape(
+        slab_count, extent // slab_count, -1
+    )
+    arrived = lax.all_to_all(stacked, "slab", split_axis=0, concat_axis=0, tiled=True)
+    arrived = arrived.reshape(
+        slab_count, extent // slab_count, local_bands, 2, row_count, 2 * half_width
+    )
+    blocked_cosine = cosine_table.reshape(slab_count, row_count, extent)
+    blocked_sine = sine_table.reshape(slab_count, row_count, extent)
     real_part, imag_part = rotate(
-        arrived[:, 0], arrived[:, 1], "bzxy,xw->bzwy", cosine_kept, sine_kept, 1.0
+        arrived[:, :, :, 0], arrived[:, :, :, 1], "szbgy,sgw->bzwy", blocked_cosine, blocked_sine, 1.0
     )
     plane_real, plane_imag = rotate(
         real_part, imag_part, "bzxy,yw->bzxw", cosine_kept, sine_kept, 1.0
@@ -132,9 +141,11 @@
     potential = project("zmy,mx->zxy", arrived, basis)
     partial_hartree = project("zxm,my->zxy", potential, basis)
     both = jnp.stack((partial_value, partial_hartree)).reshape(
-        2, row_count, band_count, band_rows, extent
+        2, row_count, plane_count, half_count * band_rows, extent
     )
-    summed = lax.all_to_all(both, "band", split_axis=2, concat_axis=2, tiled=True).sum(axis=2)
+    summed = lax.all_to_all(both, "plane", split_axis=2, concat_axis=2, tiled=True).sum(axis=2)
+    summed = summed.reshape(2, row_count, half_count, band_rows, extent)
+    summed = lax.all_to_all(summed, "half", split_axis=2, concat_axis=2, tiled=True).sum(axis=2)
     placed = lax.all_to_all(summed, "slab", split_axis=3, concat_axis=1, tiled=True)
     placed = jnp.transpose(placed, (0, 2, 3, 1))
     own_density, hartree = placed[0], placed[1]
@@ -143,10 +154,15 @@
 
 
 def solution(mesh):
+    band_count, slab_count = mesh.devices.shape
+    split_mesh = Mesh(
+        mesh.devices.reshape(band_count // 2, 2, slab_count), ("plane", "half", "slab")
+    )
+    band = ("plane", "half")
     return jax.shard_map(
         local,
-        mesh=mesh,
-        in_specs=(P("band", None, "slab", None, None), P(), P("band"), P("band", "slab", None)),
-        out_specs=(P("band", "slab", None), P("band", "slab", None)),
+        mesh=split_mesh,
+        in_specs=(P(band, None, "slab", None, None), P(), P(band), P(band, "slab", None)),
+        out_specs=(P(band, "slab", None), P(band, "slab", None)),
         check_vma=False,
     )

time: 299 us -> 241 us (0.81)
  waiting for transfers between devices: 132 us -> 74.4 us
  starting transfers between devices: 38.9 us -> 25.6 us
  matrix products: 24.1 us -> 30.8 us
  blocking collectives: 88.6 us -> 94.3 us
    all_to_all x2 -> x1, waiting for transfers between devices: 106 us -> 48.5 us  [local(): lax.all_to_all(stacked, 'slab', split_axis=0, concat_axis=0, tiled=True)]
    all_to_all x1 -> x3, blocking collectives: 43.8 us -> 76.4 us  [the longest x1 33.1 us: local(): lax.all_to_all(potential, 'slab', split_axis=0, concat_axis=1, tiled=True)]
    all_to_all x1, blocking collectives: 44.8 us -> 17.9 us  [local(): lax.all_to_all(summed, 'slab', split_axis=3, concat_axis=1, tiled=True)]
    all_to_all x2 -> x1, starting transfers between devices: 21.1 us -> 14 us  [local(): lax.all_to_all(stacked, 'slab', split_axis=0, concat_axis=0, tiled=True)]
    dot_general x18, matrix products: 20.1 us -> 27 us  [project(): return jnp.einsum(pattern, values, matrix, precision=lax.Precision.HIGHEST)]
    all_to_all x1, starting transfers between devices: 17.8 us -> 11.6 us  [local(): lax.all_to_all(spectrum, 'slab', split_axis=1, concat_axis=0, tiled=True)]
    reshape x0 -> x3, local copies, waits for them, and re-layouts: none -> 4.38 us  [the longest x1 2.3 us: local(): jnp.stack((real_part, imag_part), axis=2)]
  transfers between devices with their start and end apart: 3 -> 2, of which waited for: 3 -> 2; matrix products, arithmetic and copies ran while one was open for 0% -> 0% of each run, Pallas kernels for 0% -> 0%
where the time goes in v2:
time: 241 us
  blocking collectives  94.3 us (39%)
  waiting for transfers between devices  74.4 us (31%)
  matrix products  30.8 us (13%)
  starting transfers between devices  25.6 us (11%)
  local copies, waits for them, and re-layouts  11.9 us (5%)
  other arithmetic  2.62 us (1%)
    all_to_all x1, waiting for transfers between devices, local(): lax.all_to_all(stacked, 'slab', split_axis=0, concat_axis=0, tiled=True)  48.5 us
    all_to_all x1, blocking collectives, local(): lax.all_to_all(potential, 'slab', split_axis=0, concat_axis=1, tiled=True)  33.1 us
    dot_general x18, matrix products, project(): return jnp.einsum(pattern, values, matrix, precision=lax.Precision.HIGHEST)  27 us
    all_to_all x1, waiting for transfers between devices, local(): lax.all_to_all(spectrum, 'slab', split_axis=1, concat_axis=0, tiled=True)  25.9 us
    all_to_all x1, blocking collectives, local(): lax.all_to_all(both, 'plane', split_axis=2, concat_axis=2, tiled=True)  24.1 us
    all_to_all x1, blocking collectives, local(): lax.all_to_all(summed, 'half', split_axis=2, concat_axis=2, tiled=True)  19.2 us
    all_to_all x1, blocking collectives, local(): lax.all_to_all(summed, 'slab', split_axis=3, concat_axis=1, tiled=True)  17.9 us
    all_to_all x1, starting transfers between devices, local(): lax.all_to_all(stacked, 'slab', split_axis=0, concat_axis=0, tiled=True)  14 us
  transfers between devices with their start and end apart: 2, of which 2 were waited for; matrix products, arithmetic and copies ran while one was open for 0% of the time, Pallas kernels for 0%

profile of v2, /device:TPU:1, one launch (start us, length us, event | category | flops | bytes accessed | tf_op | source)
XLA Modules:
  0.0 240.6 jit_solution(2150423558478200854)
XLA Ops:
  0.6 0.0 copy-start
  0.6 0.8 copy-done
  1.5 0.1 fusion.146
  1.6 1.4 fusion.143
  2.9 0.1 add_convert_fusion
  3.0 0.2 copy_multiply_fusion
  3.2 0.9 fusion.12
  4.1 0.9 fusion.11
  5.0 0.9 fusion.4
  5.9 0.9 fusion.3
  6.8 0.1 pad_maximum_fusion.1
  6.9 1.2 copy.58
  8.2 2.3 reshape.164
  10.5 14.0 %all-to-all-start = ((f32[16,8,2304]{2,1,0:T(8,128)}), f32[16,8,2304]{2,1,0:T(8,128)S(1)}, u32[]{:S(2)}, u32[]{:S(2)}) async-start(f32[16,8,2304]{2,1,0:T(8,128)} %reshape.164), calls=%async_computation | async-start | bytes 2359296 | tf_op jit(solution)/shard_map/all_to_all | solution.py:112
  24.5 0.3 fusion.63
  24.8 0.3 fusion.62
  25.1 48.5 %all-to-all-done = f32[16,8,2304]{2,1,0:T(8,128)S(1)} async-done(((f32[16,8,2304]{2,1,0:T(8,128)}), f32[16,8,2304]{2,1,0:T(8,128)S(1)}, u32[]{:S(2)}, u32[]{:S(2)}) %all-to-all-start) | async-done | bytes 1179680 | tf_op jit(solution)/shard_map/all_to_all | solution.py:112
  73.5 2.1 reshape.165
  75.6 0.3 fusion.142
  75.9 2.3 convolution_bitcast_fusion
  78.2 2.3 convolution_bitcast_fusion.2
  80.6 2.3 fusion.8
  82.9 2.3 fusion.6
  85.3 2.0 fusion.17
  87.3 1.8 fusion.15
  89.1 1.8 fusion.2
  90.9 0.0 copy-start.2
  90.9 1.8 fusion.1
  92.8 0.0 copy-done.2
  92.8 3.8 %fusion.9 = f32[1,8,128,128]{3,0,2,1:T(1,128)S(1)} fusion(f32[2,8,128,128]{3,2,1,0:T(8,128)S(1)} %fusion.1, f32[2]{0:T(128)S(1)} %copy-done.2), kind=kOutput, calls=%fused_computation.27 | convolution fusion | flops 3145730 | bytes 1572872 | tf_op jit(solution)/shard_map/b,bzxy->zxy/dot_general | solution.py:126
  96.6 0.9 convolution_bitcast_fusion.6
  97.5 1.9 fusion.25
  99.4 11.6 %all-to-all-start.1 = ((f32[8,128,128]{2,0,1:T(8,128)}), f32[8,128,128]{2,0,1:T(8,128)S(1)}, u32[]{:S(2)}, u32[]{:S(2)}) async-start(f32[8,128,128]{2,0,1:T(8,128)} %fusion.25), calls=%async_computation.1 | async-start | bytes 1048576 | tf_op jit(solution)/shard_map/all_to_all | solution.py:135
  111.0 0.1 dynamic_slice.11
  111.1 0.1 dynamic-slice_multiply_fusion
  111.1 0.1 broadcast_multiply_fusion
  111.2 0.1 broadcast_add_fusion
  111.3 25.9 %all-to-all-done.1 = f32[8,128,128]{2,0,1:T(8,128)S(1)} async-done(((f32[8,128,128]{2,0,1:T(8,128)}), f32[8,128,128]{2,0,1:T(8,128)S(1)}, u32[]{:S(2)}, u32[]{:S(2)}) %all-to-all-start.1) | async-done | bytes 524320 | tf_op jit(solution)/shard_map/all_to_all | solution.py:135
  137.2 0.1 copy.67
  137.3 1.0 convolution_multiply_fusion
  138.3 0.9 fusion.42
  139.3 0.3 copy.70
  139.6 33.1 %all_to_all.69 = f32[128,8,128]{2,1,0:T(8,128)S(1)} all-to-all(f32[128,8,128]{2,1,0:T(8,128)S(1)} %copy.70), channel_id=1, replica_groups=mesh['plane'=16,'half'=2,'slab'=16] {'slab'}, dimensions={0} | all-to-all | bytes 1048576 | tf_op jit(solution)/shard_map/all_to_all | solution.py:140
  172.7 0.9 convolution_bitcast_fusion.5
  173.6 0.9 convolution_bitcast_fusion.4
  174.6 0.1 pad_maximum_fusion.2
  174.6 0.1 copy.73
  174.8 24.1 %all_to_all.70 = f32[2,8,16,8,128]{4,3,1,0,2:T(8,128)S(1)} all-to-all(f32[2,8,16,8,128]{4,3,1,0,2:T(8,128)S(1)} %copy.73), channel_id=1, replica_groups=mesh['plane'=16,'half'=2,'slab'=16] {'plane'}, dimensions={2} | all-to-all | bytes 2097152 | tf_op jit(solution)/shard_map/all_to_all | solution.py:146
  198.8 0.1 reduce_sum.18
  198.9 19.2 %all_to_all.71 = f32[2,8,2,4,128]{4,3,1,0,2:T(4,128)S(1)} all-to-all(f32[2,8,2,4,128]{4,3,1,0,2:T(4,128)S(1)} %copy.75), channel_id=1, replica_groups=mesh['plane'=16,'half'=2,'slab'=16] {'half'}, dimensions={2} | all-to-all | bytes 131072 | tf_op jit(solution)/shard_map/all_to_all | solution.py:148
  218.2 0.3 copy.76
  218.4 0.5 reshape.182
  219.0 0.0 copy-start.1
  219.0 17.9 %all_to_all.72 = f32[16,1,512]{2,1,0:T(1,128)S(1)} all-to-all(f32[16,1,512]{2,1,0:T(1,128)S(1)} %reshape.182), channel_id=1, replica_groups=mesh['plane'=16,'half'=2,'slab'=16] {'slab'}, dimensions={0} | all-to-all | bytes 65536 | tf_op jit(solution)/shard_map/all_to_all | solution.py:149
  236.9 0.5 broadcast.293
  237.4 0.7 reduce
  238.1 0.6 reshape.183
  238.8 0.3 copy.134
  239.1 0.3 all_to_all.62
  239.3 0.6 slice_bitcast_fusion.7
  239.9 0.0 copy-done.1
  239.9 0.7 fusion.76
  (10 shorter events, 0.1 us)
Async XLA Ops:
  0.6 0.8 copy-start
  10.5 63.1 %all-to-all-start = ((f32[16,8,2304]{2,1,0:T(8,128)}), f32[16,8,2304]{2,1,0:T(8,128)S(1)}, u32[]{:S(2)}, u32[]{:S(2)}) async-start(f32[16,8,2304]{2,1,0:T(8,128)} %reshape.164), calls=%async_computation | async-start | bytes 2359296 | tf_op jit(solution)/shard_map/all_to_all | solution.py:112
  90.9 1.9 copy-start.2
  99.4 37.8 %all-to-all-start.1 = ((f32[8,128,128]{2,0,1:T(8,128)}), f32[8,128,128]{2,0,1:T(8,128)S(1)}, u32[]{:S(2)}, u32[]{:S(2)}) async-start(f32[8,128,128]{2,0,1:T(8,128)} %fusion.25), calls=%async_computation.1 | async-start | bytes 1048576 | tf_op jit(solution)/shard_map/all_to_all | solution.py:135
  219.0 21.0 %copy-start.1 = (f32[4,8,128]{2,1,0:T(8,128)S(1)}, f32[4,8,128]{2,1,0:T(8,128)}, u32[]{:S(2)}) copy-start(f32[4,8,128]{2,1,0:T(8,128)} %param.7) | copy-start | bytes 49156

commit v3 on v2

--- a/solution.py
+++ b/solution.py
@@ -39,7 +39,7 @@
 
 
 def project(pattern, values, matrix):
-    return jnp.einsum(pattern, values, matrix, precision=lax.Precision.HIGHEST)
+    return jnp.einsum(pattern, values, matrix, precision=lax.Precision.HIGH)
 
 
 def rotate(real_part, imag_part, pattern, cosine_table, sine_table, direction):
@@ -123,12 +123,10 @@
     )
     factor = 1.0 / (float(extent) ** 3 * bands_all)
     weights = occupations * factor
-    partial_value = jnp.einsum(
-        "b,bzxy->zxy",
-        weights,
-        plane_real * plane_real + plane_imag * plane_imag,
-        precision=lax.Precision.HIGHEST,
-    )
+    modulus = plane_real * plane_real + plane_imag * plane_imag
+    partial_value = weights[0] * modulus[0]
+    for member in range(1, local_bands):
+        partial_value = partial_value + weights[member] * modulus[member]
     basis, frequency, weight = real_basis(extent)
     spectrum = project("zxy,mx->zmy", partial_value, basis)
     spectrum = project("zxy,my->zxm", spectrum, basis)

time: 241 us -> 231 us (0.959)
  blocking collectives: 94.3 us -> 61.2 us
  waiting for transfers between devices: 74.4 us -> 98.7 us
  matrix products: 30.8 us -> 19.6 us
  starting transfers between devices: 25.6 us -> 32.8 us
    all_to_all x1 -> x0, blocking collectives: 33.1 us -> none  [local(): lax.all_to_all(potential, 'slab', split_axis=0, concat_axis=1, tiled=True)]
    all_to_all x0 -> x1, waiting for transfers between devices: none -> 24.9 us  [local(): lax.all_to_all(potential, 'slab', split_axis=0, concat_axis=1, tiled=True)]
    dot_general x19 -> x18, matrix products: 30.8 us -> 19.6 us  [project(): return jnp.einsum(pattern, values, matrix, precision=lax.Precision.HIGH)]
    all_to_all x0 -> x1, starting transfers between devices: none -> 7.07 us  [local(): lax.all_to_all(potential, 'slab', split_axis=0, concat_axis=1, tiled=True)]
  transfers between devices with their start and end apart: 2 -> 3, of which waited for: 2 -> 3; matrix products, arithmetic and copies ran while one was open for 0% -> 1% of each run, Pallas kernels for 0% -> 0%
where the time goes in v3:
time: 231 us
  waiting for transfers between devices  98.7 us (43%)
  blocking collectives  61.2 us (26%)
  starting transfers between devices  32.8 us (14%)
  matrix products  19.6 us (8%)
  local copies, waits for them, and re-layouts  13.3 us (6%)
  other arithmetic  3.97 us (2%)
    all_to_all x1, waiting for transfers between devices, local(): lax.all_to_all(stacked, 'slab', split_axis=0, concat_axis=0, tiled=True)  47.9 us
    all_to_all x1, waiting for transfers between devices, local(): lax.all_to_all(spectrum, 'slab', split_axis=1, concat_axis=0, tiled=True)  25.9 us
    all_to_all x1, waiting for transfers between devices, local(): lax.all_to_all(potential, 'slab', split_axis=0, concat_axis=1, tiled=True)  24.9 us
    all_to_all x1, blocking collectives, local(): lax.all_to_all(both, 'plane', split_axis=2, concat_axis=2, tiled=True)  24 us
    dot_general x18, matrix products, project(): return jnp.einsum(pattern, values, matrix, precision=lax.Precision.HIGH)  19.6 us
    all_to_all x1, blocking collectives, local(): lax.all_to_all(summed, 'half', split_axis=2, concat_axis=2, tiled=True)  19.3 us
    all_to_all x1, blocking collectives, local(): lax.all_to_all(summed, 'slab', split_axis=3, concat_axis=1, tiled=True)  17.9 us
    all_to_all x1, starting transfers between devices, local(): lax.all_to_all(stacked, 'slab', split_axis=0, concat_axis=0, tiled=True)  14.2 us
  transfers between devices with their start and end apart: 3, of which 3 were waited for; matrix products, arithmetic and copies ran while one was open for 1% of the time, Pallas kernels for 0%

profile of v3, /device:TPU:1, one launch (start us, length us, event | category | flops | bytes accessed | tf_op | source)
XLA Modules:
  0.0 230.5 jit_solution(974375427154708225)
XLA Ops:
  0.6 0.0 copy-start
  0.6 0.8 copy-done
  1.5 0.1 fusion.146
  1.6 1.4 fusion.143
  2.9 0.1 add_convert_fusion
  3.0 0.2 copy_multiply_fusion
  3.2 0.6 fusion.10
  3.9 0.6 fusion.9
  4.5 0.7 fusion.4
  5.2 0.7 fusion.3
  5.9 0.1 pad_maximum_fusion.1
  5.9 1.2 copy.68
  7.2 2.3 reshape.168
  9.5 0.0 copy-start.2
  9.5 14.2 %all-to-all-start = ((f32[16,8,2304]{2,1,0:T(8,128)}), f32[16,8,2304]{2,1,0:T(8,128)S(1)}, u32[]{:S(2)}, u32[]{:S(2)}) async-start(f32[16,8,2304]{2,1,0:T(8,128)} %reshape.168), calls=%async_computation | async-start | bytes 2359296 | tf_op jit(solution)/shard_map/all_to_all | solution.py:112
  23.7 0.0 copy-done.2
  23.7 0.6 fusion.147
  24.3 0.3 fusion.65
  24.6 0.3 fusion.64
  24.8 47.9 %all-to-all-done = f32[16,8,2304]{2,1,0:T(8,128)S(1)} async-done(((f32[16,8,2304]{2,1,0:T(8,128)}), f32[16,8,2304]{2,1,0:T(8,128)S(1)}, u32[]{:S(2)}, u32[]{:S(2)}) %all-to-all-start) | async-done | bytes 1179680 | tf_op jit(solution)/shard_map/all_to_all | solution.py:112
  72.7 2.1 reshape.169
  74.8 0.3 fusion.142
  75.1 1.5 convolution_bitcast_fusion
  76.6 1.5 convolution_bitcast_fusion.2
  78.1 1.5 fusion.8
  79.6 1.5 fusion.6
  81.1 1.0 fusion.15
  82.2 1.0 fusion.13
  83.2 1.0 fusion.2
  84.2 1.2 fusion.1
  85.4 2.0 convolution_bitcast_fusion.6
  87.4 1.7 fusion.25
  89.1 11.6 %all-to-all-start.1 = ((f32[8,128,128]{2,0,1:T(8,128)}), f32[8,128,128]{2,0,1:T(8,128)S(1)}, u32[]{:S(2)}, u32[]{:S(2)}) async-start(f32[8,128,128]{2,0,1:T(8,128)} %fusion.25), calls=%async_computation.1 | async-start | bytes 1048576 | tf_op jit(solution)/shard_map/all_to_all | solution.py:133
  100.7 0.1 dynamic_slice.11
  100.8 0.1 dynamic-slice_multiply_fusion
  100.9 0.1 broadcast_multiply_fusion
  101.0 0.1 broadcast_add_fusion
  101.0 25.9 %all-to-all-done.1 = f32[8,128,128]{2,0,1:T(8,128)S(1)} async-done(((f32[8,128,128]{2,0,1:T(8,128)}), f32[8,128,128]{2,0,1:T(8,128)S(1)}, u32[]{:S(2)}, u32[]{:S(2)}) %all-to-all-start.1) | async-done | bytes 524320 | tf_op jit(solution)/shard_map/all_to_all | solution.py:133
  127.0 0.1 copy.77
  127.1 0.8 convolution_multiply_fusion
  127.9 0.7 fusion.44
  128.6 1.1 copy.80
  129.8 7.1 %all-to-all-start.2 = ((f32[128,8,128]{2,1,0:T(8,128)}), f32[128,8,128]{2,1,0:T(8,128)S(1)}, u32[]{:S(2)}, u32[]{:S(2)}) async-start(f32[128,8,128]{2,1,0:T(8,128)} %copy.80), calls=%async_computation.2 | async-start | bytes 1048576 | tf_op jit(solution)/shard_map/all_to_all | solution.py:138
  136.8 1.3 fusion.30
  138.2 24.9 %all-to-all-done.2 = f32[128,8,128]{2,1,0:T(8,128)S(1)} async-done(((f32[128,8,128]{2,1,0:T(8,128)}), f32[128,8,128]{2,1,0:T(8,128)S(1)}, u32[]{:S(2)}, u32[]{:S(2)}) %all-to-all-start.2) | async-done | bytes 524320 | tf_op jit(solution)/shard_map/all_to_all | solution.py:138
  163.0 0.7 convolution_bitcast_fusion.5
  163.8 0.7 convolution_bitcast_fusion.4
  164.5 0.1 pad_maximum_fusion.2
  164.6 0.1 copy.107
  164.7 24.0 %all_to_all.69 = f32[2,8,16,8,128]{4,3,1,0,2:T(8,128)S(1)} all-to-all(f32[2,8,16,8,128]{4,3,1,0,2:T(8,128)S(1)} %copy.107), channel_id=1, replica_groups=mesh['plane'=16,'half'=2,'slab'=16] {'plane'}, dimensions={2} | all-to-all | bytes 2097152 | tf_op jit(solution)/shard_map/all_to_all | solution.py:144
  188.7 0.1 reduce_sum.18
  188.8 19.3 %all_to_all.70 = f32[2,8,2,4,128]{4,3,1,0,2:T(4,128)S(1)} all-to-all(f32[2,8,2,4,128]{4,3,1,0,2:T(4,128)S(1)} %copy.86), channel_id=1, replica_groups=mesh['plane'=16,'half'=2,'slab'=16] {'half'}, dimensions={2} | all-to-all | bytes 131072 | tf_op jit(solution)/shard_map/all_to_all | solution.py:146
  208.1 0.3 copy.87
  208.4 0.5 reshape.184
  208.9 0.0 copy-start.1
  208.9 17.9 %all_to_all.71 = f32[16,1,512]{2,1,0:T(1,128)S(1)} all-to-all(f32[16,1,512]{2,1,0:T(1,128)S(1)} %reshape.184), channel_id=1, replica_groups=mesh['plane'=16,'half'=2,'slab'=16] {'slab'}, dimensions={0} | all-to-all | bytes 65536 | tf_op jit(solution)/shard_map/all_to_all | solution.py:147
  226.8 0.5 broadcast.296
  227.3 0.7 reduce
  228.0 0.6 reshape.185
  228.7 0.3 copy.141
  229.0 0.3 all_to_all.62
  229.3 0.6 slice_bitcast_fusion.7
  229.9 0.0 copy-done.1
  229.9 0.7 fusion.78
  (11 shorter events, 0.1 us)
Async XLA Ops:
  0.6 0.8 copy-start
  9.5 14.2 %copy-start.2 = (f32[2]{0:T(128)S(1)}, f32[2]{0:T(128)}, u32[]{:S(2)}) copy-start(f32[2]{0:T(128)} %param.6) | copy-start | bytes 28
  9.5 63.2 %all-to-all-start = ((f32[16,8,2304]{2,1,0:T(8,128)}), f32[16,8,2304]{2,1,0:T(8,128)S(1)}, u32[]{:S(2)}, u32[]{:S(2)}) async-start(f32[16,8,2304]{2,1,0:T(8,128)} %reshape.168), calls=%async_computation | async-start | bytes 2359296 | tf_op jit(solution)/shard_map/all_to_all | solution.py:112
  89.1 37.8 %all-to-all-start.1 = ((f32[8,128,128]{2,0,1:T(8,128)}), f32[8,128,128]{2,0,1:T(8,128)S(1)}, u32[]{:S(2)}, u32[]{:S(2)}) async-start(f32[8,128,128]{2,0,1:T(8,128)} %fusion.25), calls=%async_computation.1 | async-start | bytes 1048576 | tf_op jit(solution)/shard_map/all_to_all | solution.py:133
  129.8 33.3 %all-to-all-start.2 = ((f32[128,8,128]{2,1,0:T(8,128)}), f32[128,8,128]{2,1,0:T(8,128)S(1)}, u32[]{:S(2)}, u32[]{:S(2)}) async-start(f32[128,8,128]{2,1,0:T(8,128)} %copy.80), calls=%async_computation.2 | async-start | bytes 1048576 | tf_op jit(solution)/shard_map/all_to_all | solution.py:138
  208.9 21.0 %copy-start.1 = (f32[4,8,128]{2,1,0:T(8,128)S(1)}, f32[4,8,128]{2,1,0:T(8,128)}, u32[]{:S(2)}) copy-start(f32[4,8,128]{2,1,0:T(8,128)} %param.7) | copy-start | bytes 49156

commit v4 on v3

--- a/solution.py
+++ b/solution.py
@@ -38,16 +38,17 @@
     return exchange_part + correlation
 
 
-def project(pattern, values, matrix):
-    return jnp.einsum(pattern, values, matrix, precision=lax.Precision.HIGH)
+def project(pattern, values, matrix, precision=lax.Precision.HIGHEST):
+    return jnp.einsum(pattern, values, matrix, precision=precision)
 
 
 def rotate(real_part, imag_part, pattern, cosine_table, sine_table, direction):
-    new_real = project(pattern, real_part, cosine_table) - direction * project(
-        pattern, imag_part, sine_table
+    fast = lax.Precision.HIGH
+    new_real = project(pattern, real_part, cosine_table, fast) - direction * project(
+        pattern, imag_part, sine_table, fast
     )
-    new_imag = direction * project(pattern, real_part, sine_table) + project(
-        pattern, imag_part, cosine_table
+    new_imag = direction * project(pattern, real_part, sine_table, fast) + project(
+        pattern, imag_part, cosine_table, fast
     )
     return (new_real, new_imag)
 
@@ -142,10 +143,13 @@
         2, row_count, plane_count, half_count * band_rows, extent
     )
     summed = lax.all_to_all(both, "plane", split_axis=2, concat_axis=2, tiled=True).sum(axis=2)
-    summed = summed.reshape(2, row_count, half_count, band_rows, extent)
-    summed = lax.all_to_all(summed, "half", split_axis=2, concat_axis=2, tiled=True).sum(axis=2)
-    placed = lax.all_to_all(summed, "slab", split_axis=3, concat_axis=1, tiled=True)
-    placed = jnp.transpose(placed, (0, 2, 3, 1))
+    summed = summed.reshape(2, row_count, half_count, band_rows, slab_count, row_count)
+    summed = jnp.transpose(summed, (2, 4, 0, 1, 3, 5)).reshape(
+        half_count * slab_count, 2, row_count, band_rows, row_count
+    )
+    arrived = lax.all_to_all(summed, ("half", "slab"), split_axis=0, concat_axis=0, tiled=True)
+    arrived = arrived.reshape(half_count, slab_count, 2, row_count, band_rows, row_count).sum(axis=0)
+    placed = jnp.transpose(arrived, (1, 3, 4, 0, 2)).reshape(2, band_rows, row_count, extent)
     own_density, hartree = placed[0], placed[1]
     xc_potential = exchange_correlation(own_density + core_density)
     return (hartree, xc_potential)

time: 231 us -> 219 us (0.948)
  blocking collectives: 61.2 us -> 45.3 us
    all_to_all x2 -> x1, blocking collectives: 37.1 us -> 21.2 us  [local(): lax.all_to_all(summed, ('half', 'slab'), split_axis=0, concat_axis=0, til...]
where the time goes in v4:
time: 219 us
  waiting for transfers between devices  98.7 us (45%)
  blocking collectives  45.3 us (21%)
  starting transfers between devices  32.8 us (15%)
  matrix products  20.8 us (9%)
  local copies, waits for them, and re-layouts  15.5 us (7%)
  other arithmetic  4.53 us (2%)
    all_to_all x1, waiting for transfers between devices, local(): lax.all_to_all(stacked, 'slab', split_axis=0, concat_axis=0, tiled=True)  47.9 us
    all_to_all x1, waiting for transfers between devices, local(): lax.all_to_all(spectrum, 'slab', split_axis=1, concat_axis=0, tiled=True)  25.9 us
    all_to_all x1, waiting for transfers between devices, local(): lax.all_to_all(potential, 'slab', split_axis=0, concat_axis=1, tiled=True)  24.9 us
    all_to_all x1, blocking collectives, local(): lax.all_to_all(both, 'plane', split_axis=2, concat_axis=2, tiled=True)  24.1 us
    all_to_all x1, blocking collectives, local(): lax.all_to_all(summed, ('half', 'slab'), split_axis=0, concat_axis=0, til...  21.2 us
    dot_general x18, matrix products, project(): return jnp.einsum(pattern, values, matrix, precision=precision)  20.8 us
    all_to_all x1, starting transfers between devices, local(): lax.all_to_all(stacked, 'slab', split_axis=0, concat_axis=0, tiled=True)  14.2 us
    all_to_all x1, starting transfers between devices, local(): lax.all_to_all(spectrum, 'slab', split_axis=1, concat_axis=0, tiled=True)  11.6 us
  transfers between devices with their start and end apart: 3, of which 3 were waited for; matrix products, arithmetic and copies ran while one was open for 1% of the time, Pallas kernels for 0%

profile of v4, /device:TPU:1, one launch (start us, length us, event | category | flops | bytes accessed | tf_op | source)
XLA Modules:
  0.0 218.7 jit_solution(1540877597528824727)
XLA Ops:
  0.6 0.0 copy-start
  0.6 0.8 copy-done
  1.5 0.1 fusion.145
  1.6 1.4 fusion.141
  2.9 0.1 add_convert_fusion
  3.0 0.2 copy_multiply_fusion
  3.2 0.6 fusion.10
  3.9 0.6 fusion.9
  4.5 0.7 fusion.4
  5.2 0.7 fusion.3
  5.9 0.1 pad_maximum_fusion.1
  5.9 1.2 copy.49
  7.2 2.3 %reshape.179 = f32[16,8,2304]{2,1,0:T(8,128)} reshape(f32[128,2,2,8,72]{4,3,2,1,0:T(8,128)S(1)} %copy.49) | data formatting | bytes 2359296 | tf_op jit(solution)/shard_map/reshape | solution.py:110
  9.5 14.2 %all-to-all-start = ((f32[16,8,2304]{2,1,0:T(8,128)}), f32[16,8,2304]{2,1,0:T(8,128)S(1)}, u32[]{:S(2)}, u32[]{:S(2)}) async-start(f32[16,8,2304]{2,1,0:T(8,128)} %reshape.179), calls=%async_computation | async-start | bytes 2359296 | tf_op jit(solution)/shard_map/all_to_all | solution.py:113
  23.7 0.6 fusion.146
  24.3 0.3 fusion.65
  24.6 0.3 fusion.64
  24.8 47.9 %all-to-all-done = f32[16,8,2304]{2,1,0:T(8,128)S(1)} async-done(((f32[16,8,2304]{2,1,0:T(8,128)}), f32[16,8,2304]{2,1,0:T(8,128)S(1)}, u32[]{:S(2)}, u32[]{:S(2)}) %all-to-all-start) | async-done | bytes 1179680 | tf_op jit(solution)/shard_map/all_to_all | solution.py:113
  72.7 2.1 reshape.180
  74.8 0.3 fusion.140
  75.1 1.5 convolution_bitcast_fusion
  76.6 1.5 convolution_bitcast_fusion.2
  78.1 1.5 fusion.8
  79.6 1.5 fusion.6
  81.1 1.0 fusion.15
  82.2 1.0 fusion.13
  83.2 1.0 fusion.2
  84.2 1.2 fusion.1
  85.4 2.2 %convolution_bitcast_fusion.6 = f32[8,128,128]{2,1,0:T(8,128)S(1)} fusion(f32[2,8,128,128]{3,2,1,0:T(8,128)S(1)} %fusion.1, f32[]{:T(128)} %bitcast.35, f32[]{:T(128)} %bitcast, s32[128]{0:T(128)S(1)} %add_select_fusion.3, pred[128]{0:T(512)(128)(4,1)S(1)} %iota_compare_fusion), kind=kOutput, calls=%fused_computation.19 | convolution fusion | flops 201965568 | bytes 1573512 | tf_op jit(solution)/shard_map/zxy,mx->zmy/dot_general | solution.py:42
  87.6 1.9 fusion.25
  89.5 11.6 %all-to-all-start.1 = ((f32[8,128,128]{2,0,1:T(8,128)}), f32[8,128,128]{2,0,1:T(8,128)S(1)}, u32[]{:S(2)}, u32[]{:S(2)}) async-start(f32[8,128,128]{2,0,1:T(8,128)} %fusion.25), calls=%async_computation.1 | async-start | bytes 1048576 | tf_op jit(solution)/shard_map/all_to_all | solution.py:134
  101.1 0.1 dynamic_slice.11
  101.2 0.1 dynamic-slice_multiply_fusion
  101.3 0.1 broadcast_multiply_fusion
  101.4 0.1 broadcast_add_fusion
  101.4 25.9 %all-to-all-done.1 = f32[8,128,128]{2,0,1:T(8,128)S(1)} async-done(((f32[8,128,128]{2,0,1:T(8,128)}), f32[8,128,128]{2,0,1:T(8,128)S(1)}, u32[]{:S(2)}, u32[]{:S(2)}) %all-to-all-start.1) | async-done | bytes 524320 | tf_op jit(solution)/shard_map/all_to_all | solution.py:134
  127.4 0.1 copy.58
  127.5 1.0 convolution_multiply_fusion
  128.5 0.9 fusion.44
  129.4 1.1 copy.61
  130.5 7.1 %all-to-all-start.2 = ((f32[128,8,128]{2,1,0:T(8,128)}), f32[128,8,128]{2,1,0:T(8,128)S(1)}, u32[]{:S(2)}, u32[]{:S(2)}) async-start(f32[128,8,128]{2,1,0:T(8,128)} %copy.61), calls=%async_computation.2 | async-start | bytes 1048576 | tf_op jit(solution)/shard_map/all_to_all | solution.py:139
  137.6 1.3 fusion.30
  139.0 24.9 %all-to-all-done.2 = f32[128,8,128]{2,1,0:T(8,128)S(1)} async-done(((f32[128,8,128]{2,1,0:T(8,128)}), f32[128,8,128]{2,1,0:T(8,128)S(1)}, u32[]{:S(2)}, u32[]{:S(2)}) %all-to-all-start.2) | async-done | bytes 524320 | tf_op jit(solution)/shard_map/all_to_all | solution.py:139
  163.8 0.9 convolution_bitcast_fusion.5
  164.8 0.9 convolution_bitcast_fusion.4
  165.7 0.1 pad_maximum_fusion.2
  165.8 0.1 copy.88
  165.9 24.1 %all_to_all.51 = f32[2,8,16,8,128]{4,3,1,0,2:T(8,128)S(1)} all-to-all(f32[2,8,16,8,128]{4,3,1,0,2:T(8,128)S(1)} %copy.88), channel_id=1, replica_groups=mesh['plane'=16,'half'=2,'slab'=16] {'plane'}, dimensions={2} | all-to-all | bytes 2097152 | tf_op jit(solution)/shard_map/all_to_all | solution.py:145
  190.0 0.1 reduce_sum.18
  190.0 0.6 reshape.181
  190.6 0.4 copy.89
  191.0 1.1 reshape.197
  192.2 21.2 %all_to_all.52 = f32[32,1,512]{2,1,0:T(1,128)S(1)} all-to-all(f32[32,1,512]{2,1,0:T(1,128)S(1)} %reshape.197), channel_id=1, replica_groups=mesh['plane'=16,'half'=2,'slab'=16] {'half','slab'}, dimensions={0} | all-to-all | bytes 131072 | tf_op jit(solution)/shard_map/all_to_all | solution.py:150
  213.4 0.5 broadcast.296
  213.9 0.8 reduce
  214.7 1.2 reshape.198
  216.0 0.5 reduce_sum.19
  216.5 0.0 copy-start.1
  216.5 0.3 copy.91
  216.8 0.1 copy.70
  216.9 0.1 squeeze.33
  217.1 0.1 copy.69
  217.2 0.8 squeeze.32
  218.0 0.7 fusion.78
  (13 shorter events, 0.1 us)
Async XLA Ops:
  0.6 0.8 copy-start
  9.5 14.2 %copy-start.2 = (f32[2]{0:T(128)S(1)}, f32[2]{0:T(128)}, u32[]{:S(2)}) copy-start(f32[2]{0:T(128)} %param.6) | copy-start | bytes 28
  9.5 63.2 %all-to-all-start = ((f32[16,8,2304]{2,1,0:T(8,128)}), f32[16,8,2304]{2,1,0:T(8,128)S(1)}, u32[]{:S(2)}, u32[]{:S(2)}) async-start(f32[16,8,2304]{2,1,0:T(8,128)} %reshape.179), calls=%async_computation | async-start | bytes 2359296 | tf_op jit(solution)/shard_map/all_to_all | solution.py:113
  89.5 37.8 %all-to-all-start.1 = ((f32[8,128,128]{2,0,1:T(8,128)}), f32[8,128,128]{2,0,1:T(8,128)S(1)}, u32[]{:S(2)}, u32[]{:S(2)}) async-start(f32[8,128,128]{2,0,1:T(8,128)} %fusion.25), calls=%async_computation.1 | async-start | bytes 1048576 | tf_op jit(solution)/shard_map/all_to_all | solution.py:134
  130.5 33.3 %all-to-all-start.2 = ((f32[128,8,128]{2,1,0:T(8,128)}), f32[128,8,128]{2,1,0:T(8,128)S(1)}, u32[]{:S(2)}, u32[]{:S(2)}) async-start(f32[128,8,128]{2,1,0:T(8,128)} %copy.61), calls=%async_computation.2 | async-start | bytes 1048576 | tf_op jit(solution)/shard_map/all_to_all | solution.py:139
  216.5 1.5 copy-start.1

commit v5 on v4

--- a/solution.py
+++ b/solution.py
@@ -86,6 +86,17 @@
     return jnp.concatenate((low, high), axis=axis)
 
 
+def keep_slabs(values, live):
+    runs = []
+    for slab in live:
+        if runs and runs[-1][1] == slab:
+            runs[-1][1] = slab + 1
+        else:
+            runs.append([slab, slab + 1])
+    pieces = [values[start:stop] for start, stop in runs]
+    return pieces[0] if len(pieces) == 1 else jnp.concatenate(pieces, axis=0)
+
+
 def local(wave_coeffs, column_mask, occupations, core_density):
     local_bands = wave_coeffs.shape[0]
     row_count = wave_coeffs.shape[2]
@@ -116,6 +127,17 @@
     )
     blocked_cosine = cosine_table.reshape(slab_count, row_count, extent)
     blocked_sine = sine_table.reshape(slab_count, row_count, extent)
+    live = [
+        slab
+        for slab in range(slab_count)
+        if any(
+            abs((row + extent // 2) % extent - extent // 2) <= extent // 4
+            for row in range(slab * row_count, (slab + 1) * row_count)
+        )
+    ]
+    arrived = keep_slabs(arrived, live)
+    blocked_cosine = keep_slabs(blocked_cosine, live)
+    blocked_sine = keep_slabs(blocked_sine, live)
     real_part, imag_part = rotate(
         arrived[:, :, :, 0], arrived[:, :, :, 1], "szbgy,sgw->bzwy", blocked_cosine, blocked_sine, 1.0
     )
@@ -129,10 +151,10 @@
     for member in range(1, local_bands):
         partial_value = partial_value + weights[member] * modulus[member]
     basis, frequency, weight = real_basis(extent)
-    spectrum = project("zxy,mx->zmy", partial_value, basis)
-    spectrum = project("zxy,my->zxm", spectrum, basis)
-    arrived = lax.all_to_all(spectrum, "slab", split_axis=1, concat_axis=0, tiled=True)
-    spectrum = project("zxy,mz->mxy", arrived, basis)
+    spectrum = project("zxy,mx->mzy", partial_value, basis)
+    spectrum = project("xzy,my->xzm", spectrum, basis)
+    arrived = lax.all_to_all(spectrum, "slab", split_axis=0, concat_axis=1, tiled=True)
+    spectrum = project("xzy,mz->mxy", arrived, basis)
     kernel = real_kernel_block(extent, frequency, weight, slab_index * row_count, row_count)
     kernel = jnp.transpose(kernel, (2, 0, 1))
     potential = project("mxy,mz->zxy", kernel * spectrum, basis)

time: 219 us -> 217 us (level)
  matrix products: 20.8 us -> 18.5 us
    dot_general x18, matrix products: 20.8 us -> 18.5 us  [project(): return jnp.einsum(pattern, values, matrix, precision=precision)]
where the time goes in v5:
time: 217 us; the launch traced here: 216 us
  waiting for transfers between devices  98.6 us (45%)
  blocking collectives  45.3 us (21%)
  starting transfers between devices  33.1 us (15%)
  matrix products  18.5 us (9%)
  local copies, waits for them, and re-layouts  15.1 us (7%)
  other arithmetic  4.53 us (2%)
    all_to_all x1, waiting for transfers between devices, local(): lax.all_to_all(stacked, 'slab', split_axis=0, concat_axis=0, tiled=True)  47.8 us
    all_to_all x1, waiting for transfers between devices, local(): lax.all_to_all(spectrum, 'slab', split_axis=0, concat_axis=1, tiled=True)  25.9 us
    all_to_all x1, waiting for transfers between devices, local(): lax.all_to_all(potential, 'slab', split_axis=0, concat_axis=1, tiled=True)  24.9 us
    all_to_all x1, blocking collectives, local(): lax.all_to_all(both, 'plane', split_axis=2, concat_axis=2, tiled=True)  24.1 us
    all_to_all x1, blocking collectives, local(): lax.all_to_all(summed, ('half', 'slab'), split_axis=0, concat_axis=0, til...  21.2 us
    dot_general x18, matrix products, project(): return jnp.einsum(pattern, values, matrix, precision=precision)  18.5 us
    all_to_all x1, starting transfers between devices, local(): lax.all_to_all(stacked, 'slab', split_axis=0, concat_axis=0, tiled=True)  14.2 us
    all_to_all x1, starting transfers between devices, local(): lax.all_to_all(spectrum, 'slab', split_axis=0, concat_axis=1, tiled=True)  11.8 us
  transfers between devices with their start and end apart: 3, of which 3 were waited for; matrix products, arithmetic and copies ran while one was open for 1% of the time, Pallas kernels for 0%

profile of v5, /device:TPU:1, one launch (start us, length us, event | category | flops | bytes accessed | tf_op | source)
XLA Modules:
  0.0 216.1 jit_solution(10469480574871284322)
XLA Ops:
  0.6 0.0 copy-start
  0.6 0.8 copy-done
  1.5 0.1 fusion.125
  1.6 1.4 fusion.121
  2.9 0.1 add_convert_fusion
  3.0 0.2 copy_multiply_fusion
  3.2 0.6 fusion.15
  3.9 0.6 fusion.14
  4.5 0.7 fusion.4
  5.2 0.7 fusion.3
  5.9 0.1 pad_maximum_fusion.1
  5.9 1.2 copy.58
  7.2 2.3 %reshape.165 = f32[16,8,2304]{2,1,0:T(8,128)} reshape(f32[128,2,2,8,72]{4,3,2,1,0:T(8,128)S(1)} %copy.58) | data formatting | bytes 2359296 | tf_op jit(solution)/shard_map/reshape | solution.py:121
  9.5 14.2 %all-to-all-start = ((f32[16,8,2304]{2,1,0:T(8,128)}), f32[16,8,2304]{2,1,0:T(8,128)S(1)}, u32[]{:S(2)}, u32[]{:S(2)}) async-start(f32[16,8,2304]{2,1,0:T(8,128)} %reshape.165), calls=%async_computation | async-start | bytes 2359296 | tf_op jit(solution)/shard_map/all_to_all | solution.py:124
  23.7 0.3 fusion.64
  24.0 0.3 fusion.63
  24.3 0.6 fusion.126
  24.9 47.8 %all-to-all-done = f32[16,8,2304]{2,1,0:T(8,128)S(1)} async-done(((f32[16,8,2304]{2,1,0:T(8,128)}), f32[16,8,2304]{2,1,0:T(8,128)S(1)}, u32[]{:S(2)}, u32[]{:S(2)}) %all-to-all-start) | async-done | bytes 1179680 | tf_op jit(solution)/shard_map/all_to_all | solution.py:124
  72.7 0.6 slice.104
  73.4 0.4 copy.59
  73.8 0.5 slice.106
  74.3 0.3 copy.60
  74.7 1.0 convolution_bitcast_fusion
  75.7 1.0 convolution_bitcast_fusion.2
  76.7 1.0 fusion.8
  77.7 1.0 fusion.6
  78.7 1.0 fusion.20
  79.7 1.0 fusion.18
  80.7 1.0 fusion.2
  81.8 1.0 fusion.1
  82.8 2.2 %fusion.30 = f32[128,8,128]{2,0,1:T(8,128)S(1)} fusion(f32[2,8,128,128]{3,2,1,0:T(8,128)S(1)} %fusion.1, f32[]{:T(128)} %bitcast.39, f32[]{:T(128)} %bitcast, s32[128]{0:T(128)S(1)} %add_select_fusion.2, pred[128]{0:T(512)(128)(4,1)S(1)} %iota_compare_fusion), kind=kOutput, calls=%fused_computation.52 | convolution fusion | flops 201965568 | bytes 1573512 | tf_op jit(solution)/shard_map/zxy,mx->mzy/dot_general | solution.py:42
  85.0 1.9 fusion.32
  86.9 11.8 %all-to-all-start.1 = ((f32[128,8,128]{2,1,0:T(8,128)}), f32[128,8,128]{2,1,0:T(8,128)S(1)}, u32[]{:S(2)}, u32[]{:S(2)}) async-start(f32[128,8,128]{2,1,0:T(8,128)} %fusion.32), calls=%async_computation.1 | async-start | bytes 1048576 | tf_op jit(solution)/shard_map/all_to_all | solution.py:156
  98.7 0.1 dynamic_slice.11
  98.8 0.1 dynamic-slice_multiply_fusion
  98.9 0.1 broadcast_multiply_fusion
  99.0 0.1 broadcast_add_fusion
  99.0 25.9 %all-to-all-done.1 = f32[128,8,128]{2,1,0:T(8,128)S(1)} async-done(((f32[128,8,128]{2,1,0:T(8,128)}), f32[128,8,128]{2,1,0:T(8,128)S(1)}, u32[]{:S(2)}, u32[]{:S(2)}) %all-to-all-start.1) | async-done | bytes 524320 | tf_op jit(solution)/shard_map/all_to_all | solution.py:156
  125.0 1.0 convolution_multiply_fusion
  126.0 0.9 fusion.50
  126.9 1.1 copy.70
  128.0 7.1 %all-to-all-start.2 = ((f32[128,8,128]{2,1,0:T(8,128)}), f32[128,8,128]{2,1,0:T(8,128)S(1)}, u32[]{:S(2)}, u32[]{:S(2)}) async-start(f32[128,8,128]{2,1,0:T(8,128)} %copy.70), calls=%async_computation.2 | async-start | bytes 1048576 | tf_op jit(solution)/shard_map/all_to_all | solution.py:161
  135.1 1.3 fusion.37
  136.4 24.9 %all-to-all-done.2 = f32[128,8,128]{2,1,0:T(8,128)S(1)} async-done(((f32[128,8,128]{2,1,0:T(8,128)}), f32[128,8,128]{2,1,0:T(8,128)S(1)}, u32[]{:S(2)}, u32[]{:S(2)}) %all-to-all-start.2) | async-done | bytes 524320 | tf_op jit(solution)/shard_map/all_to_all | solution.py:161
  161.3 0.9 convolution_bitcast_fusion.5
  162.3 0.9 convolution_bitcast_fusion.4
  163.2 0.1 pad_maximum_fusion.3
  163.2 0.1 copy.96
  163.4 24.1 %all_to_all.51 = f32[2,8,16,8,128]{4,3,1,0,2:T(8,128)S(1)} all-to-all(f32[2,8,16,8,128]{4,3,1,0,2:T(8,128)S(1)} %copy.96), channel_id=1, replica_groups=mesh['plane'=16,'half'=2,'slab'=16] {'plane'}, dimensions={2} | all-to-all | bytes 2097152 | tf_op jit(solution)/shard_map/all_to_all | solution.py:167
  187.4 0.1 reduce_sum.18
  187.5 0.6 reshape.166
  188.1 0.4 copy.97
  188.5 1.1 reshape.182
  189.6 21.2 %all_to_all.52 = f32[32,1,512]{2,1,0:T(1,128)S(1)} all-to-all(f32[32,1,512]{2,1,0:T(1,128)S(1)} %reshape.182), channel_id=1, replica_groups=mesh['plane'=16,'half'=2,'slab'=16] {'half','slab'}, dimensions={0} | all-to-all | bytes 131072 | tf_op jit(solution)/shard_map/all_to_all | solution.py:172
  210.9 0.5 broadcast.229
  211.4 0.8 reduce
  212.2 1.2 reshape.183
  213.4 0.5 reduce_sum.19
  213.9 0.3 copy.99
  214.3 0.1 copy.79
  214.4 0.1 squeeze.33
  214.6 0.1 copy.78
  214.7 0.8 squeeze.32
  215.5 0.7 fusion.71
  (23 shorter events, 0.1 us)
Async XLA Ops:
  0.6 0.8 copy-start
  9.5 14.8 %copy-start.2 = (f32[2]{0:T(128)S(1)}, f32[2]{0:T(128)}, u32[]{:S(2)}) copy-start(f32[2]{0:T(128)} %param.6) | copy-start | bytes 28
  9.5 63.2 %all-to-all-start = ((f32[16,8,2304]{2,1,0:T(8,128)}), f32[16,8,2304]{2,1,0:T(8,128)S(1)}, u32[]{:S(2)}, u32[]{:S(2)}) async-start(f32[16,8,2304]{2,1,0:T(8,128)} %reshape.165), calls=%async_computation | async-start | bytes 2359296 | tf_op jit(solution)/shard_map/all_to_all | solution.py:124
  86.9 38.1 %all-to-all-start.1 = ((f32[128,8,128]{2,1,0:T(8,128)}), f32[128,8,128]{2,1,0:T(8,128)S(1)}, u32[]{:S(2)}, u32[]{:S(2)}) async-start(f32[128,8,128]{2,1,0:T(8,128)} %fusion.32), calls=%async_computation.1 | async-start | bytes 1048576 | tf_op jit(solution)/shard_map/all_to_all | solution.py:156
  128.0 33.3 %all-to-all-start.2 = ((f32[128,8,128]{2,1,0:T(8,128)}), f32[128,8,128]{2,1,0:T(8,128)S(1)}, u32[]{:S(2)}, u32[]{:S(2)}) async-start(f32[128,8,128]{2,1,0:T(8,128)} %copy.70), calls=%async_computation.2 | async-start | bytes 1048576 | tf_op jit(solution)/shard_map/all_to_all | solution.py:161
  213.9 1.5 copy-start.1

commit v6 on v5

--- a/solution.py
+++ b/solution.py
@@ -95,6 +95,37 @@
             runs.append([slab, slab + 1])
     pieces = [values[start:stop] for start, stop in runs]
     return pieces[0] if len(pieces) == 1 else jnp.concatenate(pieces, axis=0)
+
+
+def exchange(values, axis_name, split_axis, concat_axis):
+    count = lax.axis_size(axis_name)
+    shape = values.shape
+    chunk = shape[split_axis] // count
+    parts = values.reshape(shape[:split_axis] + (count, chunk) + shape[split_axis + 1 :])
+    parts = jnp.moveaxis(parts, split_axis, 0)
+    inner = parts.shape[1:]
+    parts = lax.all_to_all(parts.reshape(count, -1), axis_name, 0, 0, tiled=True)
+    parts = jnp.moveaxis(parts.reshape((count,) + inner), 0, concat_axis)
+    merged = list(inner)
+    merged[concat_axis] *= count
+    return parts.reshape(merged)
+
+
+def block_kernel(extent, frequency, weight, first, second):
+    rows_a = lax.dynamic_slice_in_dim(frequency, first[0], first[1], 0)
+    rows_b = lax.dynamic_slice_in_dim(frequency, second[0], second[1], 0)
+    weight_a = lax.dynamic_slice_in_dim(weight, first[0], first[1], 0)
+    weight_b = lax.dynamic_slice_in_dim(weight, second[0], second[1], 0)
+    squared = (
+        (frequency * frequency)[:, None, None]
+        + (rows_a * rows_a)[None, :, None]
+        + (rows_b * rows_b)[None, None, :]
+    )
+    length = extent * grid_spacing
+    scaled = length * length / math.pi / jnp.maximum(squared, 1).astype(jnp.float32)
+    kernel = jnp.where(squared == 0, 0.0, scaled)
+    scale = weight[:, None, None] * weight_a[None, :, None] * weight_b[None, None, :]
+    return kernel * scale / float(extent) ** 3
 
 
 def local(wave_coeffs, column_mask, occupations, core_density):
@@ -151,20 +182,28 @@
     for member in range(1, local_bands):
         partial_value = partial_value + weights[member] * modulus[member]
     basis, frequency, weight = real_basis(extent)
-    spectrum = project("zxy,mx->mzy", partial_value, basis)
-    spectrum = project("xzy,my->xzm", spectrum, basis)
-    arrived = lax.all_to_all(spectrum, "slab", split_axis=0, concat_axis=1, tiled=True)
-    spectrum = project("xzy,mz->mxy", arrived, basis)
-    kernel = real_kernel_block(extent, frequency, weight, slab_index * row_count, row_count)
-    kernel = jnp.transpose(kernel, (2, 0, 1))
-    potential = project("mxy,mz->zxy", kernel * spectrum, basis)
-    arrived = lax.all_to_all(potential, "slab", split_axis=0, concat_axis=1, tiled=True)
-    potential = project("zmy,mx->zxy", arrived, basis)
-    partial_hartree = project("zxm,my->zxy", potential, basis)
-    both = jnp.stack((partial_value, partial_hartree)).reshape(
-        2, row_count, plane_count, half_count * band_rows, extent
-    )
-    summed = lax.all_to_all(both, "plane", split_axis=2, concat_axis=2, tiled=True).sum(axis=2)
+    plane_rows = half_count * band_rows
+    spread = partial_value.reshape(row_count, plane_count, plane_rows, extent)
+    density = lax.all_to_all(spread, "plane", split_axis=1, concat_axis=1, tiled=True).sum(axis=1)
+    spectrum = project("zxy,my->zxm", density, basis)
+    spectrum = exchange(spectrum, "plane", 2, 1)
+    spectrum = project("zxm,nx->znm", spectrum, basis)
+    spectrum = exchange(spectrum, "slab", 1, 0)
+    spectrum = project("zab,mz->mab", spectrum, basis)
+    plane_index = lax.axis_index("plane")
+    kernel = block_kernel(
+        extent,
+        frequency,
+        weight,
+        (slab_index * row_count, row_count),
+        (plane_index * (extent // plane_count), extent // plane_count),
+    )
+    potential = project("mab,mz->zab", kernel * spectrum, basis)
+    potential = exchange(potential, "slab", 0, 1)
+    potential = project("znm,nx->zxm", potential, basis)
+    potential = exchange(potential, "plane", 1, 2)
+    potential = project("zxm,my->zxy", potential, basis)
+    summed = jnp.stack((density, potential))
     summed = summed.reshape(2, row_count, half_count, band_rows, slab_count, row_count)
     summed = jnp.transpose(summed, (2, 4, 0, 1, 3, 5)).reshape(
         half_count * slab_count, 2, row_count, band_rows, row_count

time: 217 us -> 201 us (0.926)
  waiting for transfers between devices: 98.6 us -> 81.1 us
  blocking collectives: 45.3 us -> 35.7 us
  starting transfers between devices: 33.1 us -> 41.1 us
  local copies, waits for them, and re-layouts: 15.1 us -> 21.4 us
  matrix products: 18.5 us -> 14.8 us
    all_to_all x2 -> x4, waiting for transfers between devices: 50.8 us -> 33.4 us  [the longest x3 21.8 us: exchange(): lax.all_to_all(parts.reshape(count, -1), axis_name, 0, 0, tiled=True)]
    all_to_all x1, blocking collectives: 24.1 us -> 13.2 us  [exchange(): lax.all_to_all(parts.reshape(count, -1), axis_name, 0, 0, tiled=True)]
    all_to_all x2 -> x4, starting transfers between devices: 18.9 us -> 26.9 us  [the longest x3 20.2 us: exchange(): lax.all_to_all(parts.reshape(count, -1), axis_name, 0, 0, tiled=True)]
    dot_general x18 -> x14, matrix products: 18.5 us -> 12.6 us  [project(): return jnp.einsum(pattern, values, matrix, precision=precision)]
    all_to_all x0 -> x7, local copies, waits for them, and re-layouts: none -> 2.82 us  [exchange(): lax.all_to_all(parts.reshape(count, -1), axis_name, 0, 0, tiled=True)]
    unnamed x0 -> x4, matrix products: none -> 2.2 us
  transfers between devices with their start and end apart: 3 -> 5, of which waited for: 3 -> 5; matrix products, arithmetic and copies ran while one was open for 1% -> 1% of each run, Pallas kernels for 0% -> 0%
where the time goes in v6:
time: 201 us; the launch traced here: 200 us
  waiting for transfers between devices  81.1 us (40%)
  starting transfers between devices  41.1 us (20%)
  blocking collectives  35.7 us (18%)
  local copies, waits for them, and re-layouts  21.4 us (11%)
  matrix products  14.8 us (7%)
  other arithmetic  4.59 us (2%)
    all_to_all x1, waiting for transfers between devices, local(): lax.all_to_all(stacked, 'slab', split_axis=0, concat_axis=0, tiled=True)  47.7 us
    all_to_all x1, blocking collectives, local(): lax.all_to_all(summed, ('half', 'slab'), split_axis=0, concat_axis=0, til...  22.5 us
    all_to_all x3, waiting for transfers between devices, exchange(): lax.all_to_all(parts.reshape(count, -1), axis_name, 0, 0, tiled=True)  21.8 us
    all_to_all x3, starting transfers between devices, exchange(): lax.all_to_all(parts.reshape(count, -1), axis_name, 0, 0, tiled=True)  20.2 us
    all_to_all x1, starting transfers between devices, local(): lax.all_to_all(stacked, 'slab', split_axis=0, concat_axis=0, tiled=True)  14.2 us
    all_to_all x1, blocking collectives, exchange(): lax.all_to_all(parts.reshape(count, -1), axis_name, 0, 0, tiled=True)  13.2 us
    dot_general x14, matrix products, project(): return jnp.einsum(pattern, values, matrix, precision=precision)  12.6 us
    all_to_all x1, waiting for transfers between devices, local(): lax.all_to_all(spread, 'plane', split_axis=1, concat_axis=1, tiled=True)  11.6 us
  transfers between devices with their start and end apart: 5, of which 5 were waited for; matrix products, arithmetic and copies ran while one was open for 1% of the time, Pallas kernels for 0%

profile of v6, /device:TPU:1, one launch (start us, length us, event | category | flops | bytes accessed | tf_op | source)
XLA Modules:
  0.0 199.9 jit_solution(38075574173171109)
XLA Ops:
  0.7 0.8 copy-done
  1.6 1.4 fusion.150
  3.2 0.6 fusion.17
  3.9 0.6 fusion.16
  4.5 0.7 fusion.4
  5.2 0.7 fusion.3
  5.9 1.2 copy.40
  7.2 2.3 %reshape.251 = f32[16,8,2304]{2,1,0:T(8,128)} reshape(f32[128,2,2,8,72]{4,3,2,1,0:T(8,128)S(1)} %copy.40) | data formatting | bytes 2359296 | tf_op jit(solution)/shard_map/reshape | solution.py:152
  9.5 14.2 %all-to-all-start = ((f32[16,8,2304]{2,1,0:T(8,128)}), f32[16,8,2304]{2,1,0:T(8,128)S(1)}, u32[]{:S(2)}, u32[]{:S(2)}) async-start(f32[16,8,2304]{2,1,0:T(8,128)} %reshape.251), calls=%async_computation | async-start | bytes 2359296 | tf_op jit(solution)/shard_map/all_to_all | solution.py:155
  23.7 0.3 fusion.90
  24.0 0.3 fusion.89
  24.4 0.6 fusion.156
  25.0 47.7 %all-to-all-done = f32[16,8,2304]{2,1,0:T(8,128)S(1)} async-done(((f32[16,8,2304]{2,1,0:T(8,128)}), f32[16,8,2304]{2,1,0:T(8,128)S(1)}, u32[]{:S(2)}, u32[]{:S(2)}) %all-to-all-start) | async-done | bytes 1179680 | tf_op jit(solution)/shard_map/all_to_all | solution.py:155
  72.7 0.6 slice.104
  73.4 0.4 copy.41
  73.8 0.5 slice.106
  74.3 0.3 copy.42
  74.7 1.0 convolution_bitcast_fusion
  75.7 1.0 convolution_bitcast_fusion.2
  76.7 1.0 fusion.8
  77.7 1.0 fusion.6
  78.7 1.0 fusion.22
  79.7 1.0 fusion.20
  80.8 1.0 fusion.2
  81.8 1.0 fusion.1
  82.8 1.4 fusion.25
  84.1 0.9 copy.49
  85.0 6.8 %all-to-all-start.1 = ((f32[8,16,8,128]{3,2,0,1:T(8,128)}), f32[8,16,8,128]{3,2,0,1:T(8,128)S(1)}, u32[]{:S(2)}, u32[]{:S(2)}) async-start(f32[8,16,8,128]{3,2,0,1:T(8,128)} %copy.49), calls=%async_computation.1 | async-start | bytes 1048576 | tf_op jit(solution)/shard_map/all_to_all | solution.py:187
  91.9 11.6 %all-to-all-done.1 = f32[8,16,8,128]{3,2,0,1:T(8,128)S(1)} async-done(((f32[8,16,8,128]{3,2,0,1:T(8,128)}), f32[8,16,8,128]{3,2,0,1:T(8,128)S(1)}, u32[]{:S(2)}, u32[]{:S(2)}) %all-to-all-start.1) | async-done | bytes 524320 | tf_op jit(solution)/shard_map/all_to_all | solution.py:187
  103.6 1.0 convolution_bitcast_fusion.5
  104.6 0.7 copy.51
  105.3 3.7 %all-to-all-start.2 = ((f32[16,1,512]{2,1,0:T(1,128)}), f32[16,1,512]{2,1,0:T(1,128)S(1)}, u32[]{:S(2)}, u32[]{:S(2)}) async-start(f32[16,1,512]{2,1,0:T(1,128)} %copy.51), calls=%async_computation.2 | async-start | bytes 65536 | tf_op jit(solution)/shard_map/all_to_all | solution.py:107
  109.1 6.2 %all-to-all-done.2 = f32[16,1,512]{2,1,0:T(1,128)S(1)} async-done(((f32[16,1,512]{2,1,0:T(1,128)}), f32[16,1,512]{2,1,0:T(1,128)S(1)}, u32[]{:S(2)}, u32[]{:S(2)}) %all-to-all-start.2) | async-done | bytes 32800 | tf_op jit(solution)/shard_map/all_to_all | solution.py:107
  115.6 0.3 reshape.253
  115.8 0.6 convolution_bitcast_fusion.9
  116.4 0.3 reshape.254
  116.9 0.7 copy.55
  117.7 13.0 %all-to-all-start.3 = ((f32[16,1,512]{2,1,0:T(1,128)}), f32[16,1,512]{2,1,0:T(1,128)S(1)}, u32[]{:S(2)}, u32[]{:S(2)}) async-start(f32[16,1,512]{2,1,0:T(1,128)} %copy.55), calls=%async_computation.3 | async-start | bytes 65536 | tf_op jit(solution)/shard_map/all_to_all | solution.py:107
  130.8 9.8 %all-to-all-done.3 = f32[16,1,512]{2,1,0:T(1,128)S(1)} async-done(((f32[16,1,512]{2,1,0:T(1,128)}), f32[16,1,512]{2,1,0:T(1,128)S(1)}, u32[]{:S(2)}, u32[]{:S(2)}) %all-to-all-start.3) | async-done | bytes 32800 | tf_op jit(solution)/shard_map/all_to_all | solution.py:107
  140.6 0.3 reshape_reshape.4
  141.1 0.6 fusion.10
  141.7 0.5 convolution_bitcast_fusion.7
  142.5 0.3 all_to_all.44
  142.8 13.2 %all_to_all.52 = f32[16,1,512]{2,1,0:T(1,128)S(1)} all-to-all(f32[16,1,512]{2,1,0:T(1,128)S(1)} %all_to_all.44), channel_id=1, replica_groups=mesh['plane'=16,'half'=2,'slab'=16] {'slab'}, dimensions={0} | all-to-all | bytes 65536 | tf_op jit(solution)/shard_map/all_to_all | solution.py:107
  156.1 0.2 copy.60
  156.3 0.3 reshape.256
  156.6 0.5 convolution_bitcast_fusion.6
  157.1 0.3 reshape.257
  157.6 0.7 copy.62
  158.3 3.5 %all-to-all-start.5 = ((f32[16,1,512]{2,1,0:T(1,128)}), f32[16,1,512]{2,1,0:T(1,128)S(1)}, u32[]{:S(2)}, u32[]{:S(2)}) async-start(f32[16,1,512]{2,1,0:T(1,128)} %copy.62), calls=%async_computation.5 | async-start | bytes 65536 | tf_op jit(solution)/shard_map/all_to_all | solution.py:107
  161.8 0.3 stack.19
  162.3 5.9 %all-to-all-done.5 = f32[16,1,512]{2,1,0:T(1,128)S(1)} async-done(((f32[16,1,512]{2,1,0:T(1,128)}), f32[16,1,512]{2,1,0:T(1,128)S(1)}, u32[]{:S(2)}, u32[]{:S(2)}) %all-to-all-start.5) | async-done | bytes 32800 | tf_op jit(solution)/shard_map/all_to_all | solution.py:107
  168.6 0.3 reshape.282
  168.8 1.0 convolution_bitcast_fusion.4
  169.9 1.1 copy.84
  171.0 1.1 reshape.286
  172.1 22.5 %all_to_all.53 = f32[32,1,512]{2,1,0:T(1,128)S(1)} all-to-all(f32[32,1,512]{2,1,0:T(1,128)S(1)} %reshape.286), channel_id=1, replica_groups=mesh['plane'=16,'half'=2,'slab'=16] {'half','slab'}, dimensions={0} | all-to-all | bytes 131072 | tf_op jit(solution)/shard_map/all_to_all | solution.py:211
  194.7 0.5 broadcast.291
  195.2 0.8 reduce.1
  196.0 1.2 reshape.287
  197.2 0.5 reduce_sum.19
  197.7 0.3 copy.86
  198.5 0.8 squeeze.32
  199.3 0.7 fusion.99
  (52 shorter events, 3.5 us)
Async XLA Ops:
  0.6 0.8 copy-start
  9.5 14.9 %copy-start.2 = (f32[2]{0:T(128)S(1)}, f32[2]{0:T(128)}, u32[]{:S(2)}) copy-start(f32[2]{0:T(128)} %param.6) | copy-start | bytes 28
  9.5 63.2 %all-to-all-start = ((f32[16,8,2304]{2,1,0:T(8,128)}), f32[16,8,2304]{2,1,0:T(8,128)S(1)}, u32[]{:S(2)}, u32[]{:S(2)}) async-start(f32[16,8,2304]{2,1,0:T(8,128)} %reshape.251), calls=%async_computation | async-start | bytes 2359296 | tf_op jit(solution)/shard_map/all_to_all | solution.py:155
  85.0 18.6 %all-to-all-start.1 = ((f32[8,16,8,128]{3,2,0,1:T(8,128)}), f32[8,16,8,128]{3,2,0,1:T(8,128)S(1)}, u32[]{:S(2)}, u32[]{:S(2)}) async-start(f32[8,16,8,128]{3,2,0,1:T(8,128)} %copy.49), calls=%async_computation.1 | async-start | bytes 1048576 | tf_op jit(solution)/shard_map/all_to_all | solution.py:187
  105.3 9.9 %all-to-all-start.2 = ((f32[16,1,512]{2,1,0:T(1,128)}), f32[16,1,512]{2,1,0:T(1,128)S(1)}, u32[]{:S(2)}, u32[]{:S(2)}) async-start(f32[16,1,512]{2,1,0:T(1,128)} %copy.51), calls=%async_computation.2 | async-start | bytes 65536 | tf_op jit(solution)/shard_map/all_to_all | solution.py:107
  117.7 22.9 %all-to-all-start.3 = ((f32[16,1,512]{2,1,0:T(1,128)}), f32[16,1,512]{2,1,0:T(1,128)S(1)}, u32[]{:S(2)}, u32[]{:S(2)}) async-start(f32[16,1,512]{2,1,0:T(1,128)} %copy.55), calls=%async_computation.3 | async-start | bytes 65536 | tf_op jit(solution)/shard_map/all_to_all | solution.py:107
  158.3 9.9 %all-to-all-start.5 = ((f32[16,1,512]{2,1,0:T(1,128)}), f32[16,1,512]{2,1,0:T(1,128)S(1)}, u32[]{:S(2)}, u32[]{:S(2)}) async-start(f32[16,1,512]{2,1,0:T(1,128)} %copy.62), calls=%async_computation.5 | async-start | bytes 65536 | tf_op jit(solution)/shard_map/all_to_all | solution.py:107
  197.7 1.5 copy-start.1

commit v7 on v6

--- a/solution.py
+++ b/solution.py
@@ -79,10 +79,10 @@
     return kernel * scale / float(extent) ** 3
 
 
-def support(values, axis, half_width):
+def support(values, axis, radius):
     extent = values.shape[axis]
-    low = lax.slice_in_dim(values, 0, half_width, axis=axis)
-    high = lax.slice_in_dim(values, extent - half_width, extent, axis=axis)
+    low = lax.slice_in_dim(values, 0, radius + 1, axis=axis)
+    high = lax.slice_in_dim(values, extent - radius, extent, axis=axis)
     return jnp.concatenate((low, high), axis=axis)
 
 
@@ -139,22 +139,20 @@
     band_rows = extent // band_count
     slab_count = lax.axis_size("slab")
     slab_index = lax.axis_index("slab")
-    half_width = -(-(extent // 4 + 1) // 4) * 4
+    radius = extent // 4
     cosine_table, sine_table = dft_tables(extent)
-    cosine_kept = support(cosine_table, 0, half_width)
-    sine_kept = support(sine_table, 0, half_width)
+    cosine_kept = support(cosine_table, 0, radius)
+    sine_kept = support(sine_table, 0, radius)
     mask_rows = lax.dynamic_slice_in_dim(column_mask, slab_index * row_count, row_count, 0)
-    mask_kept = support(mask_rows, 1, half_width).astype(jnp.float32)
-    masked = support(wave_coeffs, 3, half_width) * mask_kept[None, None, :, :, None]
+    mask_kept = support(mask_rows, 1, radius).astype(jnp.float32)
+    masked = support(wave_coeffs, 3, radius) * mask_kept[None, None, :, :, None]
     real_part, imag_part = rotate(
         masked[:, 0], masked[:, 1], "bxyz,zw->wbxy", cosine_table, sine_table, 1.0
     )
-    stacked = jnp.stack((real_part, imag_part), axis=2).reshape(
-        slab_count, extent // slab_count, -1
-    )
+    stacked = jnp.stack((real_part, imag_part), axis=2).reshape(slab_count, -1)
     arrived = lax.all_to_all(stacked, "slab", split_axis=0, concat_axis=0, tiled=True)
     arrived = arrived.reshape(
-        slab_count, extent // slab_count, local_bands, 2, row_count, 2 * half_width
+        slab_count, extent // slab_count, local_bands, 2, row_count, 2 * radius + 1
     )
     blocked_cosine = cosine_table.reshape(slab_count, row_count, extent)
     blocked_sine = sine_table.reshape(slab_count, row_count, extent)

time: 201 us -> 199 us (0.990)
  waiting for transfers between devices: 81.1 us -> 77.3 us
  local copies, waits for them, and re-layouts: 21.4 us -> 23.9 us
    all_to_all x0 -> x1, local copies, waits for them, and re-layouts: none -> 4.07 us  [local(): lax.all_to_all(stacked, 'slab', split_axis=0, concat_axis=0, tiled=True)]
    all_to_all x1, waiting for transfers between devices: 47.7 us -> 43.7 us  [local(): lax.all_to_all(stacked, 'slab', split_axis=0, concat_axis=0, tiled=True)]
    reshape x1 -> x0, local copies, waits for them, and re-layouts: 2.31 us -> none  [local(): jnp.stack((real_part, imag_part), axis=2)]
where the time goes in v7:
time: 199 us; the launch traced here: 198 us
  waiting for transfers between devices  77.3 us (39%)
  starting transfers between devices  40.5 us (20%)
  blocking collectives  35.7 us (18%)
  local copies, waits for them, and re-layouts  23.9 us (12%)
  matrix products  14.8 us (7%)
  other arithmetic  4.58 us (2%)
    all_to_all x1, waiting for transfers between devices, local(): lax.all_to_all(stacked, 'slab', split_axis=0, concat_axis=0, tiled=True)  43.7 us
    all_to_all x1, blocking collectives, local(): lax.all_to_all(summed, ('half', 'slab'), split_axis=0, concat_axis=0, til...  22.5 us
    all_to_all x3, waiting for transfers between devices, exchange(): lax.all_to_all(parts.reshape(count, -1), axis_name, 0, 0, tiled=True)  22 us
    all_to_all x3, starting transfers between devices, exchange(): lax.all_to_all(parts.reshape(count, -1), axis_name, 0, 0, tiled=True)  19.4 us
    all_to_all x1, starting transfers between devices, local(): lax.all_to_all(stacked, 'slab', split_axis=0, concat_axis=0, tiled=True)  14.2 us
    all_to_all x1, blocking collectives, exchange(): lax.all_to_all(parts.reshape(count, -1), axis_name, 0, 0, tiled=True)  13.2 us
    dot_general x14, matrix products, project(): return jnp.einsum(pattern, values, matrix, precision=precision)  12.6 us
    all_to_all x1, waiting for transfers between devices, local(): lax.all_to_all(spread, 'plane', split_axis=1, concat_axis=1, tiled=True)  11.6 us
  transfers between devices with their start and end apart: 5, of which 5 were waited for; matrix products, arithmetic and copies ran while one was open for 1% of the time, Pallas kernels for 0%

profile of v7, /device:TPU:1, one launch (start us, length us, event | category | flops | bytes accessed | tf_op | source)
XLA Modules:
  0.0 198.0 jit_solution(17595948692536056007)
XLA Ops:
  0.7 0.8 copy-done
  2.1 0.6 fusion.17
  2.8 0.6 fusion.16
  3.4 0.6 fusion.4
  4.1 0.6 fusion.3
  4.8 1.3 copy.40
  6.1 4.1 %all_to_all.48 = f32[16,1,16640]{2,1,0:T(1,128)} reshape(f32[128,2,2,8,65]{4,3,2,1,0:T(8,128)S(1)} %copy.40) | data formatting | bytes 2129920 | tf_op jit(solution)/shard_map/all_to_all | solution.py:153
  10.2 14.2 %all-to-all-start = ((f32[16,1,16640]{2,1,0:T(1,128)}), f32[16,1,16640]{2,1,0:T(1,128)S(1)}, u32[]{:S(2)}, u32[]{:S(2)}) async-start(f32[16,1,16640]{2,1,0:T(1,128)} %all_to_all.48), calls=%async_computation | async-start | bytes 2129920 | tf_op jit(solution)/shard_map/all_to_all | solution.py:153
  24.3 0.3 fusion.90
  24.7 0.3 fusion.89
  25.1 0.6 fusion.154
  25.7 43.7 %all-to-all-done = f32[16,1,16640]{2,1,0:T(1,128)S(1)} async-done(((f32[16,1,16640]{2,1,0:T(1,128)}), f32[16,1,16640]{2,1,0:T(1,128)S(1)}, u32[]{:S(2)}, u32[]{:S(2)}) %all-to-all-start) | async-done | bytes 1064992 | tf_op jit(solution)/shard_map/all_to_all | solution.py:153
  69.4 0.8 slice_reduce_fusion
  70.2 0.8 slice.106
  71.1 0.4 copy.42
  71.5 0.7 slice_reduce_fusion.1
  72.2 0.6 slice.108
  72.8 0.3 copy.43
  73.2 1.0 convolution_bitcast_fusion
  74.2 1.0 convolution_bitcast_fusion.2
  75.2 1.0 fusion.8
  76.2 1.0 fusion.6
  77.2 1.0 fusion.22
  78.2 1.0 fusion.20
  79.2 1.0 fusion.2
  80.2 1.0 fusion.1
  81.2 1.4 fusion.25
  82.6 0.8 copy.50
  83.4 7.0 %all-to-all-start.1 = ((f32[8,16,8,128]{3,2,0,1:T(8,128)}), f32[8,16,8,128]{3,2,0,1:T(8,128)S(1)}, u32[]{:S(2)}, u32[]{:S(2)}) async-start(f32[8,16,8,128]{3,2,0,1:T(8,128)} %copy.50), calls=%async_computation.1 | async-start | bytes 1048576 | tf_op jit(solution)/shard_map/all_to_all | solution.py:185
  90.6 11.6 %all-to-all-done.1 = f32[8,16,8,128]{3,2,0,1:T(8,128)S(1)} async-done(((f32[8,16,8,128]{3,2,0,1:T(8,128)}), f32[8,16,8,128]{3,2,0,1:T(8,128)S(1)}, u32[]{:S(2)}, u32[]{:S(2)}) %all-to-all-start.1) | async-done | bytes 524320 | tf_op jit(solution)/shard_map/all_to_all | solution.py:185
  102.3 1.0 convolution_bitcast_fusion.5
  103.3 0.7 copy.52
  104.0 3.5 %all-to-all-start.2 = ((f32[16,1,512]{2,1,0:T(1,128)}), f32[16,1,512]{2,1,0:T(1,128)S(1)}, u32[]{:S(2)}, u32[]{:S(2)}) async-start(f32[16,1,512]{2,1,0:T(1,128)} %copy.52), calls=%async_computation.2 | async-start | bytes 65536 | tf_op jit(solution)/shard_map/all_to_all | solution.py:107
  107.5 6.4 %all-to-all-done.2 = f32[16,1,512]{2,1,0:T(1,128)S(1)} async-done(((f32[16,1,512]{2,1,0:T(1,128)}), f32[16,1,512]{2,1,0:T(1,128)S(1)}, u32[]{:S(2)}, u32[]{:S(2)}) %all-to-all-start.2) | async-done | bytes 32800 | tf_op jit(solution)/shard_map/all_to_all | solution.py:107
  114.3 0.3 reshape.257
  114.6 0.6 convolution_bitcast_fusion.9
  115.1 0.3 reshape.258
  115.6 0.7 copy.56
  116.4 12.4 %all-to-all-start.3 = ((f32[16,1,512]{2,1,0:T(1,128)}), f32[16,1,512]{2,1,0:T(1,128)S(1)}, u32[]{:S(2)}, u32[]{:S(2)}) async-start(f32[16,1,512]{2,1,0:T(1,128)} %copy.56), calls=%async_computation.3 | async-start | bytes 65536 | tf_op jit(solution)/shard_map/all_to_all | solution.py:107
  128.8 9.8 %all-to-all-done.3 = f32[16,1,512]{2,1,0:T(1,128)S(1)} async-done(((f32[16,1,512]{2,1,0:T(1,128)}), f32[16,1,512]{2,1,0:T(1,128)S(1)}, u32[]{:S(2)}, u32[]{:S(2)}) %all-to-all-start.3) | async-done | bytes 32800 | tf_op jit(solution)/shard_map/all_to_all | solution.py:107
  138.6 0.3 reshape_reshape.4
  139.1 0.6 fusion.10
  139.7 0.5 convolution_bitcast_fusion.7
  140.5 0.3 all_to_all.49
  140.8 13.2 %all_to_all.57 = f32[16,1,512]{2,1,0:T(1,128)S(1)} all-to-all(f32[16,1,512]{2,1,0:T(1,128)S(1)} %all_to_all.49), channel_id=1, replica_groups=mesh['plane'=16,'half'=2,'slab'=16] {'slab'}, dimensions={0} | all-to-all | bytes 65536 | tf_op jit(solution)/shard_map/all_to_all | solution.py:107
  154.4 0.3 reshape.260
  154.6 0.5 convolution_bitcast_fusion.6
  155.1 0.3 reshape.261
  155.6 0.7 copy.63
  156.4 3.5 %all-to-all-start.5 = ((f32[16,1,512]{2,1,0:T(1,128)}), f32[16,1,512]{2,1,0:T(1,128)S(1)}, u32[]{:S(2)}, u32[]{:S(2)}) async-start(f32[16,1,512]{2,1,0:T(1,128)} %copy.63), calls=%async_computation.5 | async-start | bytes 65536 | tf_op jit(solution)/shard_map/all_to_all | solution.py:107
  159.9 0.3 stack.19
  160.4 5.9 %all-to-all-done.5 = f32[16,1,512]{2,1,0:T(1,128)S(1)} async-done(((f32[16,1,512]{2,1,0:T(1,128)}), f32[16,1,512]{2,1,0:T(1,128)S(1)}, u32[]{:S(2)}, u32[]{:S(2)}) %all-to-all-start.5) | async-done | bytes 32800 | tf_op jit(solution)/shard_map/all_to_all | solution.py:107
  166.6 0.3 reshape.286
  166.9 1.0 convolution_bitcast_fusion.4
  167.9 1.1 copy.85
  169.0 1.1 reshape.292
  170.2 22.5 %all_to_all.58 = f32[32,1,512]{2,1,0:T(1,128)S(1)} all-to-all(f32[32,1,512]{2,1,0:T(1,128)S(1)} %reshape.292), channel_id=1, replica_groups=mesh['plane'=16,'half'=2,'slab'=16] {'half','slab'}, dimensions={0} | all-to-all | bytes 131072 | tf_op jit(solution)/shard_map/all_to_all | solution.py:209
  192.7 0.5 broadcast.293
  193.2 0.8 reduce.5
  194.0 1.2 reshape.293
  195.3 0.5 reduce_sum.19
  195.8 0.3 copy.87
  196.6 0.8 squeeze.32
  197.3 0.7 fusion.99
  (55 shorter events, 3.9 us)
Async XLA Ops:
  0.6 0.8 copy-start
  0.6 1.1 slice-start
  0.7 1.3 slice-start.1
  10.2 14.9 %copy-start.2 = (f32[2]{0:T(128)S(1)}, f32[2]{0:T(128)}, u32[]{:S(2)}) copy-start(f32[2]{0:T(128)} %param.6) | copy-start | bytes 28
  10.2 59.2 %all-to-all-start = ((f32[16,1,16640]{2,1,0:T(1,128)}), f32[16,1,16640]{2,1,0:T(1,128)S(1)}, u32[]{:S(2)}, u32[]{:S(2)}) async-start(f32[16,1,16640]{2,1,0:T(1,128)} %all_to_all.48), calls=%async_computation | async-start | bytes 2129920 | tf_op jit(solution)/shard_map/all_to_all | solution.py:153
  83.4 18.8 %all-to-all-start.1 = ((f32[8,16,8,128]{3,2,0,1:T(8,128)}), f32[8,16,8,128]{3,2,0,1:T(8,128)S(1)}, u32[]{:S(2)}, u32[]{:S(2)}) async-start(f32[8,16,8,128]{3,2,0,1:T(8,128)} %copy.50), calls=%async_computation.1 | async-start | bytes 1048576 | tf_op jit(solution)/shard_map/all_to_all | solution.py:185
  104.0 9.9 %all-to-all-start.2 = ((f32[16,1,512]{2,1,0:T(1,128)}), f32[16,1,512]{2,1,0:T(1,128)S(1)}, u32[]{:S(2)}, u32[]{:S(2)}) async-start(f32[16,1,512]{2,1,0:T(1,128)} %copy.52), calls=%async_computation.2 | async-start | bytes 65536 | tf_op jit(solution)/shard_map/all_to_all | solution.py:107
  116.4 22.2 %all-to-all-start.3 = ((f32[16,1,512]{2,1,0:T(1,128)}), f32[16,1,512]{2,1,0:T(1,128)S(1)}, u32[]{:S(2)}, u32[]{:S(2)}) async-start(f32[16,1,512]{2,1,0:T(1,128)} %copy.56), calls=%async_computation.3 | async-start | bytes 65536 | tf_op jit(solution)/shard_map/all_to_all | solution.py:107
  156.4 9.9 %all-to-all-start.5 = ((f32[16,1,512]{2,1,0:T(1,128)}), f32[16,1,512]{2,1,0:T(1,128)S(1)}, u32[]{:S(2)}, u32[]{:S(2)}) async-start(f32[16,1,512]{2,1,0:T(1,128)} %copy.63), calls=%async_computation.5 | async-start | bytes 65536 | tf_op jit(solution)/shard_map/all_to_all | solution.py:107
  195.8 1.5 copy-start.1

commit v8 on v7

--- a/solution.py
+++ b/solution.py
@@ -146,16 +146,6 @@
     mask_rows = lax.dynamic_slice_in_dim(column_mask, slab_index * row_count, row_count, 0)
     mask_kept = support(mask_rows, 1, radius).astype(jnp.float32)
     masked = support(wave_coeffs, 3, radius) * mask_kept[None, None, :, :, None]
-    real_part, imag_part = rotate(
-        masked[:, 0], masked[:, 1], "bxyz,zw->wbxy", cosine_table, sine_table, 1.0
-    )
-    stacked = jnp.stack((real_part, imag_part), axis=2).reshape(slab_count, -1)
-    arrived = lax.all_to_all(stacked, "slab", split_axis=0, concat_axis=0, tiled=True)
-    arrived = arrived.reshape(
-        slab_count, extent // slab_count, local_bands, 2, row_count, 2 * radius + 1
-    )
-    blocked_cosine = cosine_table.reshape(slab_count, row_count, extent)
-    blocked_sine = sine_table.reshape(slab_count, row_count, extent)
     live = [
         slab
         for slab in range(slab_count)
@@ -164,21 +154,28 @@
             for row in range(slab * row_count, (slab + 1) * row_count)
         )
     ]
-    arrived = keep_slabs(arrived, live)
-    blocked_cosine = keep_slabs(blocked_cosine, live)
-    blocked_sine = keep_slabs(blocked_sine, live)
-    real_part, imag_part = rotate(
-        arrived[:, :, :, 0], arrived[:, :, :, 1], "szbgy,sgw->bzwy", blocked_cosine, blocked_sine, 1.0
-    )
-    plane_real, plane_imag = rotate(
-        real_part, imag_part, "bzxy,yw->bzxw", cosine_kept, sine_kept, 1.0
-    )
+    blocked_cosine = keep_slabs(cosine_table.reshape(slab_count, row_count, extent), live)
+    blocked_sine = keep_slabs(sine_table.reshape(slab_count, row_count, extent), live)
     factor = 1.0 / (float(extent) ** 3 * bands_all)
     weights = occupations * factor
-    modulus = plane_real * plane_real + plane_imag * plane_imag
-    partial_value = weights[0] * modulus[0]
-    for member in range(1, local_bands):
-        partial_value = partial_value + weights[member] * modulus[member]
+    partial_value = None
+    for member in range(local_bands):
+        real_part, imag_part = rotate(
+            masked[member, 0], masked[member, 1], "xyz,zw->wxy", cosine_table, sine_table, 1.0
+        )
+        stacked = jnp.stack((real_part, imag_part), axis=1).reshape(slab_count, -1)
+        arrived = lax.all_to_all(stacked, "slab", split_axis=0, concat_axis=0, tiled=True)
+        arrived = keep_slabs(
+            arrived.reshape(slab_count, extent // slab_count, 2, row_count, 2 * radius + 1), live
+        )
+        real_part, imag_part = rotate(
+            arrived[:, :, 0], arrived[:, :, 1], "szgy,sgw->zwy", blocked_cosine, blocked_sine, 1.0
+        )
+        plane_real, plane_imag = rotate(
+            real_part, imag_part, "zxy,yw->zxw", cosine_kept, sine_kept, 1.0
+        )
+        term = weights[member] * (plane_real * plane_real + plane_imag * plane_imag)
+        partial_value = term if partial_value is None else partial_value + term
     basis, frequency, weight = real_basis(extent)
     plane_rows = half_count * band_rows
     spread = partial_value.reshape(row_count, plane_count, plane_rows, extent)

time: 199 us -> 206 us (1.035)
  matrix products: 14.8 us -> 19.3 us
  starting transfers between devices: 40.5 us -> 43.4 us
    all_to_all x1 -> x2, starting transfers between devices: 14.2 us -> 21.2 us  [local(): lax.all_to_all(stacked, 'slab', split_axis=0, concat_axis=0, tiled=True)]
    dot_general x14 -> x26, matrix products: 12.6 us -> 17.1 us  [project(): return jnp.einsum(pattern, values, matrix, precision=precision)]
    all_to_all x3, starting transfers between devices: 19.4 us -> 15.5 us  [exchange(): lax.all_to_all(parts.reshape(count, -1), axis_name, 0, 0, tiled=True)]
    all_to_all x1 -> x2, waiting for transfers between devices: 43.7 us -> 44.8 us  [local(): lax.all_to_all(stacked, 'slab', split_axis=0, concat_axis=0, tiled=True)]
    all_to_all x1 -> x2, local copies, waits for them, and re-layouts: 4.07 us -> 4.49 us  [local(): lax.all_to_all(stacked, 'slab', split_axis=0, concat_axis=0, tiled=True)]
  transfers between devices with their start and end apart: 5 -> 6, of which waited for: 5 -> 6; matrix products, arithmetic and copies ran while one was open for 1% -> 3% of each run, Pallas kernels for 0% -> 0%
where the time goes in v8:
time: 206 us
  waiting for transfers between devices  78.5 us (38%)
  starting transfers between devices  43.4 us (21%)
  blocking collectives  35.7 us (17%)
  local copies, waits for them, and re-layouts  24 us (12%)
  matrix products  19.3 us (9%)
  other arithmetic  3.23 us (2%)
    all_to_all x2, waiting for transfers between devices, local(): lax.all_to_all(stacked, 'slab', split_axis=0, concat_axis=0, tiled=True)  44.8 us
    all_to_all x1, blocking collectives, local(): lax.all_to_all(summed, ('half', 'slab'), split_axis=0, concat_axis=0, til...  22.5 us
    all_to_all x3, waiting for transfers between devices, exchange(): lax.all_to_all(parts.reshape(count, -1), axis_name, 0, 0, tiled=True)  22 us
    all_to_all x2, starting transfers between devices, local(): lax.all_to_all(stacked, 'slab', split_axis=0, concat_axis=0, tiled=True)  21.2 us
    dot_general x26, matrix products, project(): return jnp.einsum(pattern, values, matrix, precision=precision)  17.1 us
    all_to_all x3, starting transfers between devices, exchange(): lax.all_to_all(parts.reshape(count, -1), axis_name, 0, 0, tiled=True)  15.5 us
    all_to_all x1, blocking collectives, exchange(): lax.all_to_all(parts.reshape(count, -1), axis_name, 0, 0, tiled=True)  13.2 us
    all_to_all x1, waiting for transfers between devices, local(): lax.all_to_all(spread, 'plane', split_axis=1, concat_axis=1, tiled=True)  11.6 us
  transfers between devices with their start and end apart: 6, of which 6 were waited for; matrix products, arithmetic and copies ran while one was open for 3% of the time, Pallas kernels for 0%

profile of v8, /device:TPU:1, one launch (start us, length us, event | category | flops | bytes accessed | tf_op | source)
XLA Modules:
  0.0 205.5 jit_solution(9576700306870670321)
XLA Ops:
  0.7 0.8 copy-done
  2.1 0.5 fusion.34
  2.6 0.5 fusion.35
  3.2 0.5 fusion.12
  3.7 0.5 fusion.13
  4.3 0.5 copy.29
  4.8 2.2 %all_to_all.56 = f32[16,1,8320]{2,1,0:T(1,128)} reshape(f32[128,2,8,65]{3,2,1,0:T(8,128)S(1)} %copy.29) | data formatting | bytes 1064960 | tf_op jit(solution)/shard_map/all_to_all | solution.py:167
  7.0 14.0 %all-to-all-start = ((f32[16,1,8320]{2,1,0:T(1,128)}), f32[16,1,8320]{2,1,0:T(1,128)S(1)}, u32[]{:S(2)}, u32[]{:S(2)}) async-start(f32[16,1,8320]{2,1,0:T(1,128)} %all_to_all.56), calls=%async_computation | async-start | bytes 1064960 | tf_op jit(solution)/shard_map/all_to_all | solution.py:167
  21.3 0.5 fusion.36
  21.9 0.5 fusion.10
  22.4 0.5 fusion.37
  22.9 0.5 fusion.11
  23.5 0.5 copy.35
  24.1 2.3 %all_to_all.57 = f32[16,1,8320]{2,1,0:T(1,128)} reshape(f32[128,2,8,65]{3,2,1,0:T(8,128)S(1)} %copy.35) | data formatting | bytes 1064960 | tf_op jit(solution)/shard_map/all_to_all | solution.py:167
  26.3 21.3 %all-to-all-done = f32[16,1,8320]{2,1,0:T(1,128)S(1)} async-done(((f32[16,1,8320]{2,1,0:T(1,128)}), f32[16,1,8320]{2,1,0:T(1,128)S(1)}, u32[]{:S(2)}, u32[]{:S(2)}) %all-to-all-start) | async-done | bytes 532512 | tf_op jit(solution)/shard_map/all_to_all | solution.py:167
  47.6 7.1 %all-to-all-start.1 = ((f32[16,1,8320]{2,1,0:T(1,128)}), f32[16,1,8320]{2,1,0:T(1,128)S(1)}, u32[]{:S(2)}, u32[]{:S(2)}) async-start(f32[16,1,8320]{2,1,0:T(1,128)} %all_to_all.57), calls=%async_computation.1 | async-start | bytes 1064960 | tf_op jit(solution)/shard_map/all_to_all | solution.py:167
  55.2 0.6 fusion.204
  55.8 0.4 slice_reduce_fusion.1
  57.7 23.6 %all-to-all-done.1 = f32[16,1,8320]{2,1,0:T(1,128)S(1)} async-done(((f32[16,1,8320]{2,1,0:T(1,128)}), f32[16,1,8320]{2,1,0:T(1,128)S(1)}, u32[]{:S(2)}, u32[]{:S(2)}) %all-to-all-start.1) | async-done | bytes 532512 | tf_op jit(solution)/shard_map/all_to_all | solution.py:167
  81.3 0.4 slice_reduce_fusion
  83.1 0.6 convolution_bitcast_fusion.4
  83.7 0.6 convolution_bitcast_fusion.6
  84.3 0.6 convolution_bitcast_fusion
  84.9 0.6 convolution_bitcast_fusion.2
  85.5 0.6 fusion.15
  86.1 0.6 fusion.19
  86.7 0.6 fusion.119
  87.3 0.6 fusion.120
  87.9 0.6 fusion.121
  88.5 0.6 fusion.122
  89.1 0.6 fusion.17
  89.7 0.6 fusion.21
  90.3 0.6 fusion.5
  90.9 0.6 fusion.9
  91.5 1.5 fusion.8
  93.0 1.2 fusion.4
  94.3 0.8 copy.39
  95.1 6.8 %all-to-all-start.2 = ((f32[8,16,8,128]{3,2,0,1:T(8,128)}), f32[8,16,8,128]{3,2,0,1:T(8,128)S(1)}, u32[]{:S(2)}, u32[]{:S(2)}) async-start(f32[8,16,8,128]{3,2,0,1:T(8,128)} %copy.39), calls=%async_computation.2 | async-start | bytes 1048576 | tf_op jit(solution)/shard_map/all_to_all | solution.py:182
  102.0 11.6 %all-to-all-done.2 = f32[8,16,8,128]{3,2,0,1:T(8,128)S(1)} async-done(((f32[8,16,8,128]{3,2,0,1:T(8,128)}), f32[8,16,8,128]{3,2,0,1:T(8,128)S(1)}, u32[]{:S(2)}, u32[]{:S(2)}) %all-to-all-start.2) | async-done | bytes 524320 | tf_op jit(solution)/shard_map/all_to_all | solution.py:182
  113.7 1.0 convolution_bitcast_fusion.9
  114.7 0.7 copy.41
  115.4 3.5 %all-to-all-start.3 = ((f32[16,1,512]{2,1,0:T(1,128)}), f32[16,1,512]{2,1,0:T(1,128)S(1)}, u32[]{:S(2)}, u32[]{:S(2)}) async-start(f32[16,1,512]{2,1,0:T(1,128)} %copy.41), calls=%async_computation.3 | async-start | bytes 65536 | tf_op jit(solution)/shard_map/all_to_all | solution.py:107
  118.9 6.4 %all-to-all-done.3 = f32[16,1,512]{2,1,0:T(1,128)S(1)} async-done(((f32[16,1,512]{2,1,0:T(1,128)}), f32[16,1,512]{2,1,0:T(1,128)S(1)}, u32[]{:S(2)}, u32[]{:S(2)}) %all-to-all-start.3) | async-done | bytes 32800 | tf_op jit(solution)/shard_map/all_to_all | solution.py:107
  125.9 0.6 convolution_bitcast_fusion.13
  127.0 0.7 copy.45
  127.7 8.6 %all-to-all-start.4 = ((f32[16,1,512]{2,1,0:T(1,128)}), f32[16,1,512]{2,1,0:T(1,128)S(1)}, u32[]{:S(2)}, u32[]{:S(2)}) async-start(f32[16,1,512]{2,1,0:T(1,128)} %copy.45), calls=%async_computation.4 | async-start | bytes 65536 | tf_op jit(solution)/shard_map/all_to_all | solution.py:107
  136.4 9.8 %all-to-all-done.4 = f32[16,1,512]{2,1,0:T(1,128)S(1)} async-done(((f32[16,1,512]{2,1,0:T(1,128)}), f32[16,1,512]{2,1,0:T(1,128)S(1)}, u32[]{:S(2)}, u32[]{:S(2)}) %all-to-all-start.4) | async-done | bytes 32800 | tf_op jit(solution)/shard_map/all_to_all | solution.py:107
  146.7 0.6 fusion.23
  147.3 0.5 convolution_bitcast_fusion.11
  148.4 13.2 %all_to_all.67 = f32[16,1,512]{2,1,0:T(1,128)S(1)} all-to-all(f32[16,1,512]{2,1,0:T(1,128)S(1)} %all_to_all.58), channel_id=1, replica_groups=mesh['plane'=16,'half'=2,'slab'=16] {'slab'}, dimensions={0} | all-to-all | bytes 65536 | tf_op jit(solution)/shard_map/all_to_all | solution.py:107
  162.2 0.5 convolution_bitcast_fusion.10
  163.3 0.7 copy.52
  164.0 3.5 %all-to-all-start.6 = ((f32[16,1,512]{2,1,0:T(1,128)}), f32[16,1,512]{2,1,0:T(1,128)S(1)}, u32[]{:S(2)}, u32[]{:S(2)}) async-start(f32[16,1,512]{2,1,0:T(1,128)} %copy.52), calls=%async_computation.6 | async-start | bytes 65536 | tf_op jit(solution)/shard_map/all_to_all | solution.py:107
  168.0 5.9 %all-to-all-done.6 = f32[16,1,512]{2,1,0:T(1,128)S(1)} async-done(((f32[16,1,512]{2,1,0:T(1,128)}), f32[16,1,512]{2,1,0:T(1,128)S(1)}, u32[]{:S(2)}, u32[]{:S(2)}) %all-to-all-start.6) | async-done | bytes 32800 | tf_op jit(solution)/shard_map/all_to_all | solution.py:107
  174.5 1.0 convolution_bitcast_fusion.8
  175.5 1.1 copy.72
  176.6 1.1 reshape.305
  177.7 22.5 %all_to_all.68 = f32[32,1,512]{2,1,0:T(1,128)S(1)} all-to-all(f32[32,1,512]{2,1,0:T(1,128)S(1)} %reshape.305), channel_id=1, replica_groups=mesh['plane'=16,'half'=2,'slab'=16] {'half','slab'}, dimensions={0} | all-to-all | bytes 131072 | tf_op jit(solution)/shard_map/all_to_all | solution.py:206
  200.3 0.5 broadcast.313
  200.8 0.8 reduce.9
  201.6 1.2 reshape.306
  202.8 0.5 reduce_sum.19
  204.1 0.8 squeeze.46
  204.9 0.7 fusion.125
  (77 shorter events, 9.8 us)
Async XLA Ops:
  0.6 0.8 copy-start
  0.6 1.1 slice-start
  0.7 1.3 slice-start.1
  7.0 40.6 %all-to-all-start = ((f32[16,1,8320]{2,1,0:T(1,128)}), f32[16,1,8320]{2,1,0:T(1,128)S(1)}, u32[]{:S(2)}, u32[]{:S(2)}) async-start(f32[16,1,8320]{2,1,0:T(1,128)} %all_to_all.56), calls=%async_computation | async-start | bytes 1064960 | tf_op jit(solution)/shard_map/all_to_all | solution.py:167
  24.0 31.2 %copy-start.2 = (f32[2]{0:T(128)S(1)}, f32[2]{0:T(128)}, u32[]{:S(2)}) copy-start(f32[2]{0:T(128)} %param.6) | copy-start | bytes 28
  47.6 33.7 %all-to-all-start.1 = ((f32[16,1,8320]{2,1,0:T(1,128)}), f32[16,1,8320]{2,1,0:T(1,128)S(1)}, u32[]{:S(2)}, u32[]{:S(2)}) async-start(f32[16,1,8320]{2,1,0:T(1,128)} %all_to_all.57), calls=%async_computation.1 | async-start | bytes 1064960 | tf_op jit(solution)/shard_map/all_to_all | solution.py:167
  95.1 18.6 %all-to-all-start.2 = ((f32[8,16,8,128]{3,2,0,1:T(8,128)}), f32[8,16,8,128]{3,2,0,1:T(8,128)S(1)}, u32[]{:S(2)}, u32[]{:S(2)}) async-start(f32[8,16,8,128]{3,2,0,1:T(8,128)} %copy.39), calls=%async_computation.2 | async-start | bytes 1048576 | tf_op jit(solution)/shard_map/all_to_all | solution.py:182
  115.4 9.9 %all-to-all-start.3 = ((f32[16,1,512]{2,1,0:T(1,128)}), f32[16,1,512]{2,1,0:T(1,128)S(1)}, u32[]{:S(2)}, u32[]{:S(2)}) async-start(f32[16,1,512]{2,1,0:T(1,128)} %copy.41), calls=%async_computation.3 | async-start | bytes 65536 | tf_op jit(solution)/shard_map/all_to_all | solution.py:107
  127.7 18.4 %all-to-all-start.4 = ((f32[16,1,512]{2,1,0:T(1,128)}), f32[16,1,512]{2,1,0:T(1,128)S(1)}, u32[]{:S(2)}, u32[]{:S(2)}) async-start(f32[16,1,512]{2,1,0:T(1,128)} %copy.45), calls=%async_computation.4 | async-start | bytes 65536 | tf_op jit(solution)/shard_map/all_to_all | solution.py:107
  164.0 9.9 %all-to-all-start.6 = ((f32[16,1,512]{2,1,0:T(1,128)}), f32[16,1,512]{2,1,0:T(1,128)S(1)}, u32[]{:S(2)}, u32[]{:S(2)}) async-start(f32[16,1,512]{2,1,0:T(1,128)} %copy.52), calls=%async_computation.6 | async-start | bytes 65536 | tf_op jit(solution)/shard_map/all_to_all | solution.py:107
  203.4 1.5 copy-start.1

commit v9 on v7

--- a/solution.py
+++ b/solution.py
@@ -196,11 +196,11 @@
         (slab_index * row_count, row_count),
         (plane_index * (extent // plane_count), extent // plane_count),
     )
-    potential = project("mab,mz->zab", kernel * spectrum, basis)
+    potential = project("mab,mz->zab", kernel * spectrum, basis, lax.Precision.HIGH)
     potential = exchange(potential, "slab", 0, 1)
-    potential = project("znm,nx->zxm", potential, basis)
+    potential = project("znm,nx->zxm", potential, basis, lax.Precision.HIGH)
     potential = exchange(potential, "plane", 1, 2)
-    potential = project("zxm,my->zxy", potential, basis)
+    potential = project("zxm,my->zxy", potential, basis, lax.Precision.HIGH)
     summed = jnp.stack((density, potential))
     summed = summed.reshape(2, row_count, half_count, band_rows, slab_count, row_count)
     summed = jnp.transpose(summed, (2, 4, 0, 1, 3, 5)).reshape(

time: 199 us -> 198 us (level)
  no operation moved by 1% of the time
where the time goes in v9:
time: 198 us
  waiting for transfers between devices  77.3 us (39%)
  starting transfers between devices  40.5 us (20%)
  blocking collectives  35.7 us (18%)
  local copies, waits for them, and re-layouts  23.9 us (12%)
  matrix products  14.4 us (7%)
  other arithmetic  4.58 us (2%)
    all_to_all x1, waiting for transfers between devices, local(): lax.all_to_all(stacked, 'slab', split_axis=0, concat_axis=0, tiled=True)  43.7 us
    all_to_all x1, blocking collectives, local(): lax.all_to_all(summed, ('half', 'slab'), split_axis=0, concat_axis=0, til...  22.5 us
    all_to_all x3, waiting for transfers between devices, exchange(): lax.all_to_all(parts.reshape(count, -1), axis_name, 0, 0, tiled=True)  22 us
    all_to_all x3, starting transfers between devices, exchange(): lax.all_to_all(parts.reshape(count, -1), axis_name, 0, 0, tiled=True)  19.4 us
    all_to_all x1, starting transfers between devices, local(): lax.all_to_all(stacked, 'slab', split_axis=0, concat_axis=0, tiled=True)  14.2 us
    all_to_all x1, blocking collectives, exchange(): lax.all_to_all(parts.reshape(count, -1), axis_name, 0, 0, tiled=True)  13.2 us
    dot_general x14, matrix products, project(): return jnp.einsum(pattern, values, matrix, precision=precision)  12.2 us
    all_to_all x1, waiting for transfers between devices, local(): lax.all_to_all(spread, 'plane', split_axis=1, concat_axis=1, tiled=True)  11.6 us
  transfers between devices with their start and end apart: 5, of which 5 were waited for; matrix products, arithmetic and copies ran while one was open for 1% of the time, Pallas kernels for 0%

profile of v9, /device:TPU:1, one launch (start us, length us, event | category | flops | bytes accessed | tf_op | source)
XLA Modules:
  0.0 197.6 jit_solution(513230057552819811)
XLA Ops:
  0.7 0.8 copy-done
  2.1 0.6 fusion.17
  2.8 0.6 fusion.16
  3.4 0.6 fusion.4
  4.1 0.6 fusion.3
  4.8 1.3 copy.40
  6.1 4.1 %all_to_all.48 = f32[16,1,16640]{2,1,0:T(1,128)} reshape(f32[128,2,2,8,65]{4,3,2,1,0:T(8,128)S(1)} %copy.40) | data formatting | bytes 2129920 | tf_op jit(solution)/shard_map/all_to_all | solution.py:153
  10.2 14.2 %all-to-all-start = ((f32[16,1,16640]{2,1,0:T(1,128)}), f32[16,1,16640]{2,1,0:T(1,128)S(1)}, u32[]{:S(2)}, u32[]{:S(2)}) async-start(f32[16,1,16640]{2,1,0:T(1,128)} %all_to_all.48), calls=%async_computation | async-start | bytes 2129920 | tf_op jit(solution)/shard_map/all_to_all | solution.py:153
  24.3 0.3 fusion.90
  24.7 0.3 fusion.89
  25.1 0.6 fusion.154
  25.7 43.7 %all-to-all-done = f32[16,1,16640]{2,1,0:T(1,128)S(1)} async-done(((f32[16,1,16640]{2,1,0:T(1,128)}), f32[16,1,16640]{2,1,0:T(1,128)S(1)}, u32[]{:S(2)}, u32[]{:S(2)}) %all-to-all-start) | async-done | bytes 1064992 | tf_op jit(solution)/shard_map/all_to_all | solution.py:153
  69.4 0.8 slice_reduce_fusion
  70.2 0.8 slice.106
  71.1 0.4 copy.42
  71.5 0.7 slice_reduce_fusion.1
  72.2 0.6 slice.108
  72.8 0.3 copy.43
  73.2 1.0 convolution_bitcast_fusion
  74.2 1.0 convolution_bitcast_fusion.2
  75.2 1.0 fusion.8
  76.2 1.0 fusion.6
  77.2 1.0 fusion.22
  78.2 1.0 fusion.20
  79.2 1.0 fusion.2
  80.2 1.0 fusion.1
  81.2 1.4 fusion.25
  82.6 0.8 copy.50
  83.4 7.0 %all-to-all-start.1 = ((f32[8,16,8,128]{3,2,0,1:T(8,128)}), f32[8,16,8,128]{3,2,0,1:T(8,128)S(1)}, u32[]{:S(2)}, u32[]{:S(2)}) async-start(f32[8,16,8,128]{3,2,0,1:T(8,128)} %copy.50), calls=%async_computation.1 | async-start | bytes 1048576 | tf_op jit(solution)/shard_map/all_to_all | solution.py:185
  90.6 11.6 %all-to-all-done.1 = f32[8,16,8,128]{3,2,0,1:T(8,128)S(1)} async-done(((f32[8,16,8,128]{3,2,0,1:T(8,128)}), f32[8,16,8,128]{3,2,0,1:T(8,128)S(1)}, u32[]{:S(2)}, u32[]{:S(2)}) %all-to-all-start.1) | async-done | bytes 524320 | tf_op jit(solution)/shard_map/all_to_all | solution.py:185
  102.3 1.0 convolution_bitcast_fusion.5
  103.3 0.7 copy.52
  104.0 3.5 %all-to-all-start.2 = ((f32[16,1,512]{2,1,0:T(1,128)}), f32[16,1,512]{2,1,0:T(1,128)S(1)}, u32[]{:S(2)}, u32[]{:S(2)}) async-start(f32[16,1,512]{2,1,0:T(1,128)} %copy.52), calls=%async_computation.2 | async-start | bytes 65536 | tf_op jit(solution)/shard_map/all_to_all | solution.py:107
  107.5 6.4 %all-to-all-done.2 = f32[16,1,512]{2,1,0:T(1,128)S(1)} async-done(((f32[16,1,512]{2,1,0:T(1,128)}), f32[16,1,512]{2,1,0:T(1,128)S(1)}, u32[]{:S(2)}, u32[]{:S(2)}) %all-to-all-start.2) | async-done | bytes 32800 | tf_op jit(solution)/shard_map/all_to_all | solution.py:107
  114.3 0.3 reshape.257
  114.6 0.6 convolution_bitcast_fusion.9
  115.1 0.3 reshape.258
  115.6 0.7 copy.56
  116.4 12.4 %all-to-all-start.3 = ((f32[16,1,512]{2,1,0:T(1,128)}), f32[16,1,512]{2,1,0:T(1,128)S(1)}, u32[]{:S(2)}, u32[]{:S(2)}) async-start(f32[16,1,512]{2,1,0:T(1,128)} %copy.56), calls=%async_computation.3 | async-start | bytes 65536 | tf_op jit(solution)/shard_map/all_to_all | solution.py:107
  128.8 9.8 %all-to-all-done.3 = f32[16,1,512]{2,1,0:T(1,128)S(1)} async-done(((f32[16,1,512]{2,1,0:T(1,128)}), f32[16,1,512]{2,1,0:T(1,128)S(1)}, u32[]{:S(2)}, u32[]{:S(2)}) %all-to-all-start.3) | async-done | bytes 32800 | tf_op jit(solution)/shard_map/all_to_all | solution.py:107
  138.6 0.3 reshape_reshape.4
  139.1 0.6 fusion.10
  139.7 0.5 convolution_bitcast_fusion.7
  140.5 0.3 all_to_all.49
  140.8 13.2 %all_to_all.57 = f32[16,1,512]{2,1,0:T(1,128)S(1)} all-to-all(f32[16,1,512]{2,1,0:T(1,128)S(1)} %all_to_all.49), channel_id=1, replica_groups=mesh['plane'=16,'half'=2,'slab'=16] {'slab'}, dimensions={0} | all-to-all | bytes 65536 | tf_op jit(solution)/shard_map/all_to_all | solution.py:107
  154.3 0.3 reshape.260
  154.6 0.5 convolution_bitcast_fusion.6
  155.1 0.3 reshape.261
  155.6 0.7 copy.63
  156.3 3.5 %all-to-all-start.5 = ((f32[16,1,512]{2,1,0:T(1,128)}), f32[16,1,512]{2,1,0:T(1,128)S(1)}, u32[]{:S(2)}, u32[]{:S(2)}) async-start(f32[16,1,512]{2,1,0:T(1,128)} %copy.63), calls=%async_computation.5 | async-start | bytes 65536 | tf_op jit(solution)/shard_map/all_to_all | solution.py:107
  159.8 0.3 stack.19
  160.3 5.9 %all-to-all-done.5 = f32[16,1,512]{2,1,0:T(1,128)S(1)} async-done(((f32[16,1,512]{2,1,0:T(1,128)}), f32[16,1,512]{2,1,0:T(1,128)S(1)}, u32[]{:S(2)}, u32[]{:S(2)}) %all-to-all-start.5) | async-done | bytes 32800 | tf_op jit(solution)/shard_map/all_to_all | solution.py:107
  166.6 0.3 reshape.286
  166.8 0.6 convolution_bitcast_fusion.4
  167.5 1.1 copy.85
  168.6 1.1 reshape.292
  169.8 22.5 %all_to_all.58 = f32[32,1,512]{2,1,0:T(1,128)S(1)} all-to-all(f32[32,1,512]{2,1,0:T(1,128)S(1)} %reshape.292), channel_id=1, replica_groups=mesh['plane'=16,'half'=2,'slab'=16] {'half','slab'}, dimensions={0} | all-to-all | bytes 131072 | tf_op jit(solution)/shard_map/all_to_all | solution.py:209
  192.3 0.5 broadcast.293
  192.8 0.8 reduce.5
  193.6 1.2 reshape.293
  194.9 0.5 reduce_sum.19
  195.4 0.3 copy.87
  196.2 0.8 squeeze.32
  196.9 0.7 fusion.99
  (55 shorter events, 3.9 us)
Async XLA Ops:
  0.6 0.8 copy-start
  0.6 1.1 slice-start
  0.7 1.3 slice-start.1
  10.2 14.9 %copy-start.2 = (f32[2]{0:T(128)S(1)}, f32[2]{0:T(128)}, u32[]{:S(2)}) copy-start(f32[2]{0:T(128)} %param.6) | copy-start | bytes 28
  10.2 59.2 %all-to-all-start = ((f32[16,1,16640]{2,1,0:T(1,128)}), f32[16,1,16640]{2,1,0:T(1,128)S(1)}, u32[]{:S(2)}, u32[]{:S(2)}) async-start(f32[16,1,16640]{2,1,0:T(1,128)} %all_to_all.48), calls=%async_computation | async-start | bytes 2129920 | tf_op jit(solution)/shard_map/all_to_all | solution.py:153
  83.4 18.8 %all-to-all-start.1 = ((f32[8,16,8,128]{3,2,0,1:T(8,128)}), f32[8,16,8,128]{3,2,0,1:T(8,128)S(1)}, u32[]{:S(2)}, u32[]{:S(2)}) async-start(f32[8,16,8,128]{3,2,0,1:T(8,128)} %copy.50), calls=%async_computation.1 | async-start | bytes 1048576 | tf_op jit(solution)/shard_map/all_to_all | solution.py:185
  104.0 9.9 %all-to-all-start.2 = ((f32[16,1,512]{2,1,0:T(1,128)}), f32[16,1,512]{2,1,0:T(1,128)S(1)}, u32[]{:S(2)}, u32[]{:S(2)}) async-start(f32[16,1,512]{2,1,0:T(1,128)} %copy.52), calls=%async_computation.2 | async-start | bytes 65536 | tf_op jit(solution)/shard_map/all_to_all | solution.py:107
  116.4 22.2 %all-to-all-start.3 = ((f32[16,1,512]{2,1,0:T(1,128)}), f32[16,1,512]{2,1,0:T(1,128)S(1)}, u32[]{:S(2)}, u32[]{:S(2)}) async-start(f32[16,1,512]{2,1,0:T(1,128)} %copy.56), calls=%async_computation.3 | async-start | bytes 65536 | tf_op jit(solution)/shard_map/all_to_all | solution.py:107
  156.3 9.9 %all-to-all-start.5 = ((f32[16,1,512]{2,1,0:T(1,128)}), f32[16,1,512]{2,1,0:T(1,128)S(1)}, u32[]{:S(2)}, u32[]{:S(2)}) async-start(f32[16,1,512]{2,1,0:T(1,128)} %copy.63), calls=%async_computation.5 | async-start | bytes 65536 | tf_op jit(solution)/shard_map/all_to_all | solution.py:107
  195.4 1.5 copy-start.1

commit v10 on v9

--- a/solution.py
+++ b/solution.py
@@ -207,10 +207,14 @@
         half_count * slab_count, 2, row_count, band_rows, row_count
     )
     arrived = lax.all_to_all(summed, ("half", "slab"), split_axis=0, concat_axis=0, tiled=True)
-    arrived = arrived.reshape(half_count, slab_count, 2, row_count, band_rows, row_count).sum(axis=0)
-    placed = jnp.transpose(arrived, (1, 3, 4, 0, 2)).reshape(2, band_rows, row_count, extent)
-    own_density, hartree = placed[0], placed[1]
-    xc_potential = exchange_correlation(own_density + core_density)
+    arrived = arrived.reshape(half_count, slab_count, 2, row_count, band_rows, row_count)
+
+    def place(which):
+        total = arrived[:, :, which].sum(axis=0)
+        return jnp.transpose(total, (2, 3, 0, 1)).reshape(band_rows, row_count, extent)
+
+    hartree = place(1)
+    xc_potential = exchange_correlation(place(0) + core_density)
     return (hartree, xc_potential)
 
 

time: 198 us -> 198 us (level)
  no operation moved by 1% of the time
where the time goes in v10:
time: 198 us; the launch traced here: 197 us
  waiting for transfers between devices  77.3 us (39%)
  starting transfers between devices  40.5 us (20%)
  blocking collectives  35.7 us (18%)
  local copies, waits for them, and re-layouts  23.7 us (12%)
  matrix products  14.4 us (7%)
  other arithmetic  4.45 us (2%)
    all_to_all x1, waiting for transfers between devices, local(): lax.all_to_all(stacked, 'slab', split_axis=0, concat_axis=0, tiled=True)  43.7 us
    all_to_all x1, blocking collectives, local(): lax.all_to_all(summed, ('half', 'slab'), split_axis=0, concat_axis=0, til...  22.5 us
    all_to_all x3, waiting for transfers between devices, exchange(): lax.all_to_all(parts.reshape(count, -1), axis_name, 0, 0, tiled=True)  22 us
    all_to_all x3, starting transfers between devices, exchange(): lax.all_to_all(parts.reshape(count, -1), axis_name, 0, 0, tiled=True)  19.3 us
    all_to_all x1, starting transfers between devices, local(): lax.all_to_all(stacked, 'slab', split_axis=0, concat_axis=0, tiled=True)  14.2 us
    all_to_all x1, blocking collectives, exchange(): lax.all_to_all(parts.reshape(count, -1), axis_name, 0, 0, tiled=True)  13.2 us
    dot_general x14, matrix products, project(): return jnp.einsum(pattern, values, matrix, precision=precision)  12.2 us
    all_to_all x1, waiting for transfers between devices, local(): lax.all_to_all(spread, 'plane', split_axis=1, concat_axis=1, tiled=True)  11.6 us
  transfers between devices with their start and end apart: 5, of which 5 were waited for; matrix products, arithmetic and copies ran while one was open for 1% of the time, Pallas kernels for 0%

profile of v10, /device:TPU:1, one launch (start us, length us, event | category | flops | bytes accessed | tf_op | source)
XLA Modules:
  0.0 197.2 jit_solution(15255331411378853805)
XLA Ops:
  0.7 0.8 copy-done
  2.1 0.6 fusion.17
  2.8 0.6 fusion.16
  3.4 0.6 fusion.4
  4.1 0.6 fusion.3
  4.8 1.3 copy.40
  6.1 4.1 %all_to_all.48 = f32[16,1,16640]{2,1,0:T(1,128)} reshape(f32[128,2,2,8,65]{4,3,2,1,0:T(8,128)S(1)} %copy.40) | data formatting | bytes 2129920 | tf_op jit(solution)/shard_map/all_to_all | solution.py:153
  10.2 14.2 %all-to-all-start = ((f32[16,1,16640]{2,1,0:T(1,128)}), f32[16,1,16640]{2,1,0:T(1,128)S(1)}, u32[]{:S(2)}, u32[]{:S(2)}) async-start(f32[16,1,16640]{2,1,0:T(1,128)} %all_to_all.48), calls=%async_computation | async-start | bytes 2129920 | tf_op jit(solution)/shard_map/all_to_all | solution.py:153
  24.3 0.3 fusion.90
  24.7 0.3 fusion.89
  25.1 0.6 fusion.153
  25.7 43.7 %all-to-all-done = f32[16,1,16640]{2,1,0:T(1,128)S(1)} async-done(((f32[16,1,16640]{2,1,0:T(1,128)}), f32[16,1,16640]{2,1,0:T(1,128)S(1)}, u32[]{:S(2)}, u32[]{:S(2)}) %all-to-all-start) | async-done | bytes 1064992 | tf_op jit(solution)/shard_map/all_to_all | solution.py:153
  69.4 0.8 slice_reduce_fusion.2
  70.2 0.8 slice.104
  71.0 0.4 copy.42
  71.5 0.7 slice_reduce_fusion.3
  72.2 0.6 slice.106
  72.8 0.3 copy.43
  73.1 1.0 convolution_bitcast_fusion
  74.2 1.0 convolution_bitcast_fusion.2
  75.2 1.0 fusion.8
  76.2 1.0 fusion.6
  77.2 1.0 fusion.22
  78.2 1.0 fusion.20
  79.2 1.0 fusion.2
  80.2 1.0 fusion.1
  81.2 1.4 fusion.25
  82.6 0.8 copy.50
  83.4 7.0 %all-to-all-start.1 = ((f32[8,16,8,128]{3,2,0,1:T(8,128)}), f32[8,16,8,128]{3,2,0,1:T(8,128)S(1)}, u32[]{:S(2)}, u32[]{:S(2)}) async-start(f32[8,16,8,128]{3,2,0,1:T(8,128)} %copy.50), calls=%async_computation.1 | async-start | bytes 1048576 | tf_op jit(solution)/shard_map/all_to_all | solution.py:185
  90.6 11.6 %all-to-all-done.1 = f32[8,16,8,128]{3,2,0,1:T(8,128)S(1)} async-done(((f32[8,16,8,128]{3,2,0,1:T(8,128)}), f32[8,16,8,128]{3,2,0,1:T(8,128)S(1)}, u32[]{:S(2)}, u32[]{:S(2)}) %all-to-all-start.1) | async-done | bytes 524320 | tf_op jit(solution)/shard_map/all_to_all | solution.py:185
  102.3 1.0 convolution_bitcast_fusion.5
  103.3 0.7 copy.52
  104.0 3.5 %all-to-all-start.2 = ((f32[16,1,512]{2,1,0:T(1,128)}), f32[16,1,512]{2,1,0:T(1,128)S(1)}, u32[]{:S(2)}, u32[]{:S(2)}) async-start(f32[16,1,512]{2,1,0:T(1,128)} %copy.52), calls=%async_computation.2 | async-start | bytes 65536 | tf_op jit(solution)/shard_map/all_to_all | solution.py:107
  107.5 6.4 %all-to-all-done.2 = f32[16,1,512]{2,1,0:T(1,128)S(1)} async-done(((f32[16,1,512]{2,1,0:T(1,128)}), f32[16,1,512]{2,1,0:T(1,128)S(1)}, u32[]{:S(2)}, u32[]{:S(2)}) %all-to-all-start.2) | async-done | bytes 32800 | tf_op jit(solution)/shard_map/all_to_all | solution.py:107
  114.0 0.2 copy.54
  114.3 0.3 reshape.258
  114.6 0.6 convolution_bitcast_fusion.9
  115.1 0.3 reshape.259
  115.6 0.7 copy.56
  116.4 12.4 %all-to-all-start.3 = ((f32[16,1,512]{2,1,0:T(1,128)}), f32[16,1,512]{2,1,0:T(1,128)S(1)}, u32[]{:S(2)}, u32[]{:S(2)}) async-start(f32[16,1,512]{2,1,0:T(1,128)} %copy.56), calls=%async_computation.3 | async-start | bytes 65536 | tf_op jit(solution)/shard_map/all_to_all | solution.py:107
  128.8 9.8 %all-to-all-done.3 = f32[16,1,512]{2,1,0:T(1,128)S(1)} async-done(((f32[16,1,512]{2,1,0:T(1,128)}), f32[16,1,512]{2,1,0:T(1,128)S(1)}, u32[]{:S(2)}, u32[]{:S(2)}) %all-to-all-start.3) | async-done | bytes 32800 | tf_op jit(solution)/shard_map/all_to_all | solution.py:107
  138.6 0.3 reshape_reshape.4
  139.1 0.6 fusion.10
  139.7 0.5 convolution_bitcast_fusion.7
  140.5 0.3 all_to_all.49
  140.8 13.2 %all_to_all.57 = f32[16,1,512]{2,1,0:T(1,128)S(1)} all-to-all(f32[16,1,512]{2,1,0:T(1,128)S(1)} %all_to_all.49), channel_id=1, replica_groups=mesh['plane'=16,'half'=2,'slab'=16] {'slab'}, dimensions={0} | all-to-all | bytes 65536 | tf_op jit(solution)/shard_map/all_to_all | solution.py:107
  154.3 0.3 reshape.261
  154.6 0.5 convolution_bitcast_fusion.6
  155.1 0.3 reshape.262
  155.6 0.7 copy.63
  156.3 3.5 %all-to-all-start.5 = ((f32[16,1,512]{2,1,0:T(1,128)}), f32[16,1,512]{2,1,0:T(1,128)S(1)}, u32[]{:S(2)}, u32[]{:S(2)}) async-start(f32[16,1,512]{2,1,0:T(1,128)} %copy.63), calls=%async_computation.5 | async-start | bytes 65536 | tf_op jit(solution)/shard_map/all_to_all | solution.py:107
  159.8 0.3 stack.19
  160.3 5.9 %all-to-all-done.5 = f32[16,1,512]{2,1,0:T(1,128)S(1)} async-done(((f32[16,1,512]{2,1,0:T(1,128)}), f32[16,1,512]{2,1,0:T(1,128)S(1)}, u32[]{:S(2)}, u32[]{:S(2)}) %all-to-all-start.5) | async-done | bytes 32800 | tf_op jit(solution)/shard_map/all_to_all | solution.py:107
  166.6 0.3 reshape.289
  166.8 0.6 convolution_bitcast_fusion.4
  167.5 1.1 copy.86
  168.6 1.1 reshape.295
  169.8 22.5 %all_to_all.58 = f32[32,1,512]{2,1,0:T(1,128)S(1)} all-to-all(f32[32,1,512]{2,1,0:T(1,128)S(1)} %reshape.295), channel_id=1, replica_groups=mesh['plane'=16,'half'=2,'slab'=16] {'half','slab'}, dimensions={0} | all-to-all | bytes 131072 | tf_op jit(solution)/shard_map/all_to_all | solution.py:209
  192.3 0.5 broadcast.293
  192.8 0.8 reduce.7
  193.6 1.2 reshape.296
  194.9 0.4 slice_reduce_fusion
  195.8 0.8 reshape.267
  196.6 0.7 fusion.99
  (53 shorter events, 3.7 us)
Async XLA Ops:
  0.6 0.8 copy-start
  0.6 1.1 slice-start
  0.7 1.3 slice-start.1
  10.2 14.9 %copy-start.2 = (f32[2]{0:T(128)S(1)}, f32[2]{0:T(128)}, u32[]{:S(2)}) copy-start(f32[2]{0:T(128)} %param.6) | copy-start | bytes 28
  10.2 59.2 %all-to-all-start = ((f32[16,1,16640]{2,1,0:T(1,128)}), f32[16,1,16640]{2,1,0:T(1,128)S(1)}, u32[]{:S(2)}, u32[]{:S(2)}) async-start(f32[16,1,16640]{2,1,0:T(1,128)} %all_to_all.48), calls=%async_computation | async-start | bytes 2129920 | tf_op jit(solution)/shard_map/all_to_all | solution.py:153
  83.4 18.8 %all-to-all-start.1 = ((f32[8,16,8,128]{3,2,0,1:T(8,128)}), f32[8,16,8,128]{3,2,0,1:T(8,128)S(1)}, u32[]{:S(2)}, u32[]{:S(2)}) async-start(f32[8,16,8,128]{3,2,0,1:T(8,128)} %copy.50), calls=%async_computation.1 | async-start | bytes 1048576 | tf_op jit(solution)/shard_map/all_to_all | solution.py:185
  104.0 9.9 %all-to-all-start.2 = ((f32[16,1,512]{2,1,0:T(1,128)}), f32[16,1,512]{2,1,0:T(1,128)S(1)}, u32[]{:S(2)}, u32[]{:S(2)}) async-start(f32[16,1,512]{2,1,0:T(1,128)} %copy.52), calls=%async_computation.2 | async-start | bytes 65536 | tf_op jit(solution)/shard_map/all_to_all | solution.py:107
  116.4 22.2 %all-to-all-start.3 = ((f32[16,1,512]{2,1,0:T(1,128)}), f32[16,1,512]{2,1,0:T(1,128)S(1)}, u32[]{:S(2)}, u32[]{:S(2)}) async-start(f32[16,1,512]{2,1,0:T(1,128)} %copy.56), calls=%async_computation.3 | async-start | bytes 65536 | tf_op jit(solution)/shard_map/all_to_all | solution.py:107
  156.3 9.9 %all-to-all-start.5 = ((f32[16,1,512]{2,1,0:T(1,128)}), f32[16,1,512]{2,1,0:T(1,128)S(1)}, u32[]{:S(2)}, u32[]{:S(2)}) async-start(f32[16,1,512]{2,1,0:T(1,128)} %copy.63), calls=%async_computation.5 | async-start | bytes 65536 | tf_op jit(solution)/shard_map/all_to_all | solution.py:107
  195.3 1.3 copy-start.1
